TPU v7x, 1024 devices: a whole 4x8x16 slice. The times are simulated.
1024 devices in a mesh: seq: 64 (over z, x), ctx: 16 (over y, core).
Axes of the slice: x: 4, y: 8, z: 16, core: 2. Of those that a mesh axis runs over, the one named last changes fastest.
Arguments:
- queries: bfloat16 [16, 4096, 8192], P('ctx', 'seq'), may hold values from -36 to 36
- keys: bfloat16 [16, 4096, 1024], P('ctx', 'seq'), may hold values from -6 to 6
- values: bfloat16 [16, 4096, 1024], P('ctx', 'seq'), may hold values from -6 to 6
- columns: int32 [64, 8], replicated, may hold values from 0 to 511, as said below
- offsets: int32 [64, 4], replicated, may hold values from 0 to 7, as said below
Outputs:
- attended: bfloat16 [16, 4096, 8192], P('ctx', 'seq')
Inputs may be any that keep to these rules, and one draw needn't show every extreme that they name: `columns`: each row holds 8 different block numbers. For every head, at most 2 of its blocks lie in one range of 32 blocks that starts at a multiple of 32, and some range holds exactly 2 of them. Each row holds 4 different offsets, the first of them 0.
All inputs are finite; a program needn't handle non-finite values.
Results may differ from a plain program's by a relative error of at most 0.0046.
Values may be sent and summed in bfloat16 or wider, within the bound.
No kernel may reach another device: no remote copies, remote signals or barrier semaphores. Data moves between devices by JAX's collectives and lax.ppermute only.
A program may use at most 32 MiB of HBM per device.

v0:
```python
import math

import jax
import jax.numpy as jnp
from jax import lax
from jax.sharding import PartitionSpec as P

BLK = 128


def from_behind(block, axis, distance):
    devices = range(lax.axis_size(axis))
    route = [(i - distance, i) for i in devices if i - distance in devices]
    return lax.ppermute(block, axis, route)


def shards(queries, keys, values, columns, offsets):
    tokens_dev = queries.shape[1]
    seq_count = lax.axis_size("seq")
    head_dim = queries.shape[2] // seq_count
    kv_heads = keys.shape[2] // head_dim
    group_size = seq_count // kv_heads
    vertical_count = columns.shape[1]
    slash_count = offsets.shape[1]
    local_queries = queries.reshape(tokens_dev, seq_count, head_dim)
    local_pairs = jnp.concatenate(
        [
            keys.reshape(tokens_dev, kv_heads, 1, head_dim),
            values.reshape(tokens_dev, kv_heads, 1, head_dim),
        ],
        axis=3,
    )
    local_pairs = jnp.broadcast_to(
        local_pairs, (tokens_dev, kv_heads, group_size, 2 * head_dim)
    ).reshape(tokens_dev, seq_count, 2 * head_dim)
    head_queries = lax.all_to_all(local_queries, "seq", split_axis=1, concat_axis=0, tiled=True)
    head_pairs = lax.all_to_all(local_pairs, "seq", split_axis=1, concat_axis=0, tiled=True)
    range_len = tokens_dev * seq_count
    blocks_slab = range_len // BLK
    head_queries = head_queries.reshape(range_len, head_dim)
    own_pairs = head_pairs.reshape(range_len, 2 * head_dim)
    own_blocks = own_pairs.reshape(blocks_slab, BLK, 2 * head_dim)
    head_index = lax.axis_index("seq")
    range_index = lax.axis_index("ctx")
    vertical = lax.dynamic_index_in_dim(columns, head_index, 0, keepdims=False)
    slashes = lax.dynamic_index_in_dim(offsets, head_index, 0, keepdims=False)
    first_block = range_index * blocks_slab
    local_index = vertical - first_block
    owned_mask = (local_index >= 0) & (local_index < blocks_slab)
    clipped_local = jnp.clip(local_index, 0, blocks_slab - 1)
    taken_blocks = own_blocks[clipped_local]
    slot_table = jnp.where(owned_mask[:, None, None], taken_blocks, jnp.zeros((), jnp.bfloat16))
    vertical_pairs = lax.psum(slot_table, "ctx").astype(jnp.float32).astype(jnp.bfloat16)
    previous = from_behind(own_pairs, "ctx", 1)
    previous_blocks = previous.shape[0] // BLK
    key_pool = jnp.concatenate(
        [previous.reshape(previous_blocks, BLK, 2 * head_dim), own_blocks, vertical_pairs], axis=0
    )
    pool_size = key_pool.shape[0]
    pool_base = first_block - previous_blocks
    query_index = first_block + jnp.arange(blocks_slab, dtype=jnp.int32)
    slash_blocks = query_index[:, None] - slashes[None, :]
    repeated = jnp.any(slash_blocks[:, :, None] == vertical[None, None, :], axis=2)
    candidates = jnp.concatenate(
        [jnp.broadcast_to(vertical[None, :], (blocks_slab, vertical_count)), slash_blocks], axis=1
    )
    usable = jnp.concatenate(
        [jnp.ones((blocks_slab, vertical_count), dtype=bool), jnp.logical_not(repeated)], axis=1
    )
    usable = usable & (candidates >= 0) & (candidates <= query_index[:, None])
    vertical_slots = jnp.broadcast_to(
        (previous_blocks + blocks_slab + jnp.arange(vertical_count, dtype=jnp.int32))[None, :],
        (blocks_slab, vertical_count),
    )
    pool_index = jnp.concatenate([vertical_slots, slash_blocks - pool_base], axis=1)
    pool_index = jnp.clip(pool_index, 0, pool_size - 1)
    group_blocks = math.gcd(blocks_slab, max(1, 512 // BLK))
    group_count = blocks_slab // group_blocks
    candidate_count = vertical_count + slash_count
    row_index = jnp.arange(BLK, dtype=jnp.int32)
    score_scale = 1.0 / math.sqrt(head_dim)

    def one_group(inputs):
        group_queries, group_index, group_candidates, group_usable, group_blocks_index = inputs
        nearby = key_pool[group_index].reshape(group_blocks, candidate_count * BLK, 2 * head_dim)
        nearby_keys = nearby[:, :, :head_dim]
        nearby_values = nearby[:, :, head_dim:]
        scores = (
            jnp.einsum(
                "gqd,gkd->gqk", group_queries, nearby_keys, preferred_element_type=jnp.float32
            )
            * score_scale
        )
        visible = (group_candidates < group_blocks_index[:, None])[:, None, :, None] | (
            row_index[None, None, None, :] <= row_index[None, :, None, None]
        )
        allowed = (group_usable[:, None, :, None] & visible).reshape(group_blocks, BLK, -1)
        scores = jnp.where(allowed, scores, -1e30)
        row_max = jnp.max(scores, axis=2, keepdims=True)
        weights = jnp.where(allowed, jnp.exp(scores - row_max), 0.0)
        denominator = jnp.sum(weights, axis=2, keepdims=True)
        weighted = jnp.einsum(
            "gqk,gkd->gqd",
            weights.astype(jnp.bfloat16),
            nearby_values,
            preferred_element_type=jnp.float32,
        )
        return (weighted / denominator).astype(jnp.bfloat16)

    grouped = (
        head_queries.reshape(group_count, group_blocks, BLK, head_dim),
        pool_index.reshape(group_count, group_blocks, candidate_count),
        candidates.reshape(group_count, group_blocks, candidate_count),
        usable.reshape(group_count, group_blocks, candidate_count),
        query_index.reshape(group_count, group_blocks),
    )
    head_output = lax.map(one_group, grouped).reshape(range_len, 1, head_dim)
    returned = lax.all_to_all(head_output, "seq", split_axis=0, concat_axis=1, tiled=True)
    return returned.reshape(1, tokens_dev, seq_count * head_dim)


def solution(mesh):
    placed = (P("ctx", "seq", None), P("ctx", "seq", None), P("ctx", "seq", None), P(), P())
    return jax.shard_map(
        shards, mesh=mesh, in_specs=placed, out_specs=P("ctx", "seq", None), check_vma=False
    )
```

profile of v0, /device:TPU:26, one launch (start us, length us, event | category | flops | bytes accessed | tf_op | source)
XLA Modules:
  0.0 465.6 jit_solution(11283696805813293026)
XLA Ops:
  10.1 22.3 %all-to-all-start.1 = ((bf16[64,64,256]{2,0,1:T(8,128)(2,1)}), bf16[64,64,256]{2,0,1:T(8,128)(2,1)S(1)}, u32[]{:S(2)}, u32[]{:S(2)}) async-start(bf16[64,64,256]{2,0,1:T(8,128)(2,1)} %bitcast.102), calls=%async_computation.1 | async-start | bytes 4194304 | tf_op jit(solution)/shard_map/all_to_all | solution.py:37
  34.5 98.1 %all-to-all-done.1 = bf16[64,64,256]{2,0,1:T(8,128)(2,1)S(1)} async-done(((bf16[64,64,256]{2,0,1:T(8,128)(2,1)}), bf16[64,64,256]{2,0,1:T(8,128)(2,1)S(1)}, u32[]{:S(2)}, u32[]{:S(2)}) %all-to-all-start.1) | async-done | bytes 2097184 | tf_op jit(solution)/shard_map/all_to_all | solution.py:37
  132.6 6.1 %all-to-all-start = ((bf16[64,64,128]{2,0,1:T(8,128)(2,1)}), bf16[64,64,128]{2,0,1:T(8,128)(2,1)}, u32[]{:S(2)}, u32[]{:S(2)}) async-start(bf16[64,64,128]{2,0,1:T(8,128)(2,1)} %copy.32), calls=%async_computation | async-start | bytes 2097152 | tf_op jit(solution)/shard_map/all_to_all | solution.py:36
  144.4 126.7 %all-reduce.3.cloned.1.call-done = bf16[8,128,256]{2,1,0:T(8,128)(2,1)} async-done(((bf16[8,128,256]{2,1,0:T(8,128)(2,1)}), bf16[8,128,256]{2,1,0:T(8,128)(2,1)}) %all-reduce.3.cloned.1.call-update) | async-done | bytes 524304 | tf_op jit(solution)/shard_map/psum | solution.py:53
  271.0 3.8 pad_maximum_fusion
  274.8 104.7 %while.11 = (s32[]{:T(128)}, bf16[8,4,128,128]{3,2,1,0:T(8,128)(2,1)}, pred[8,4,12]{2,1,0:T(4,128)(4,1)}, s32[8,4,12]{2,1,0:T(4,128)}, s32[8,4]{1,0:T(8,128)S(1)...) while((s32[]{:T(128)}, ...), condition=%wide.region_5.6_spmd.clone, body=%wide.region_2.5_spmd.clone.sunk | while | flops 410667712 | bytes 13933261 | solution.py:117
  277.8 3.1 gather_fusion
  281.3 4.0 fusion.58
  290.9 3.1 gather_fusion
  294.4 4.0 fusion.58
  303.9 3.1 gather_fusion
  307.5 4.0 fusion.58
  317.0 3.1 gather_fusion
  320.6 4.0 fusion.58
  330.1 3.1 gather_fusion
  333.6 4.0 fusion.58
  343.2 3.1 gather_fusion
  346.7 4.0 fusion.58
  356.3 3.1 gather_fusion
  359.8 4.0 fusion.58
  369.4 3.1 gather_fusion
  372.9 4.0 fusion.58
  380.1 2.7 reduce.6
  383.1 72.5 %all_to_all.45 = bf16[64,2,4096]{2,1,0:T(2,128)(2,1)S(1)} all-to-all(bf16[64,2,4096]{2,1,0:T(2,128)(2,1)S(1)} %reshape.271), channel_id=1, replica_groups=mesh['seq'=64,'ctx'=16] {'seq'}, dimensions={0} | all-to-all | bytes 2097152 | tf_op jit(solution)/shard_map/all_to_all | solution.py:118
  (148 shorter events, 62.8 us)
Async XLA Ops:
  6.5 134.2 %copy-start = (s32[64,4]{0,1:T(4,128)S(1)}, s32[64,4]{0,1:T(4,128)}, u32[]{:S(2)}) copy-start(s32[64,4]{0,1:T(4,128)} %param.11) | copy-start | bytes 3076
  8.5 23.9 %copy-start.1 = (bf16[1,64,8192]{2,1,0:T(8,128)(2,1)S(1)}, bf16[1,64,8192]{2,1,0:T(8,128)(2,1)}, u32[]{:S(2)}) copy-start(bf16[1,64,8192]{2,1,0:T(8,128)(2,1)} %param.7) | copy-start | bytes 3145732
  10.1 122.4 %all-to-all-start.1 = ((bf16[64,64,256]{2,0,1:T(8,128)(2,1)}), bf16[64,64,256]{2,0,1:T(8,128)(2,1)S(1)}, u32[]{:S(2)}, u32[]{:S(2)}) async-start(bf16[64,64,256]{2,0,1:T(8,128)(2,1)} %bitcast.102), calls=%async_computation.1 | async-start | bytes 4194304 | tf_op jit(solution)/shard_map/all_to_all | solution.py:37
  32.5 108.5 %copy-start.2 = (s32[64,8]{0,1:T(8,128)S(1)}, s32[64,8]{0,1:T(8,128)}, u32[]{:S(2)}) copy-start(s32[64,8]{0,1:T(8,128)} %param.10) | copy-start | bytes 6148
  132.6 142.2 %all-to-all-start = ((bf16[64,64,128]{2,0,1:T(8,128)(2,1)}), bf16[64,64,128]{2,0,1:T(8,128)(2,1)}, u32[]{:S(2)}, u32[]{:S(2)}) async-start(bf16[64,64,128]{2,0,1:T(8,128)(2,1)} %copy.32), calls=%async_computation | async-start | bytes 2097152 | tf_op jit(solution)/shard_map/all_to_all | solution.py:36
  138.7 132.3 %all-reduce.3.cloned.1.call-start = ((), (), s32[]{:S(2)}) async-start(), calls=%async_computation.3 | async-start | bytes 1048576 | tf_op jit(solution)/shard_map/psum | solution.py:53
  138.8 132.3 %collective-permute-start = (bf16[4096,256]{1,0:T(8,128)(2,1)S(1)}, bf16[4096,256]{1,0:T(8,128)(2,1)}, u32[]{:S(2)}, u32[]{:S(2)}) collective-permute-start(bf16[4096,256]{1,0:T(8,128)(2,1)S(1)} %bitcast.99), channel_id=1, source_target_pairs={{0,1},{1,2},{2,3},{3,4},{4,5},{5,6},{6,7},{7,8},{8,9},{9,10},{10,1... | collective-permute-start | bytes 6291464 | tf_op jit(solution)/shard_map/ppermute | solution.py:14
Sparse Core Ops, SparseCore 0:
  143.1 127.8 all-reduce.2
where the time goes:
time: 467 us; the launch traced here: 466 us
  waiting for transfers between devices  225 us (48%)
  blocking collectives  72.5 us (16%)
  matrix products  53.1 us (11%)
  local copies, waits for them, and re-layouts  50.8 us (11%)
  starting transfers between devices  30.4 us (7%)
  other arithmetic  20.2 us (4%)
  between operations  13.6 us (3%)
    psum x1, waiting for transfers between devices, shards(): lax.psum(slot_table, 'ctx').astype(jnp.float32).astype(jnp.bfloat16)  127 us
    all_to_all x1, waiting for transfers between devices, shards(): lax.all_to_all(local_pairs, 'seq', split_axis=1, concat_axis=0, tiled=True)  98.1 us
    all_to_all x1, blocking collectives, shards(): lax.all_to_all(head_output, 'seq', split_axis=0, concat_axis=1, tiled=True)  72.5 us
    sub x8, matrix products, one_group(): weights = jnp.where(allowed, jnp.exp(scores - row_max), 0.0)  32.1 us
    gather x8, local copies, waits for them, and re-layouts, one_group(): key_pool[group_index]  24.7 us
    all_to_all x1, starting transfers between devices, shards(): lax.all_to_all(local_pairs, 'seq', split_axis=1, concat_axis=0, tiled=True)  22.3 us
    dot_general x8, matrix products, one_group(): jnp.einsum('gqk,gkd->gqd', weights.astype(jnp.bfloat16), nearby_values, p...  21 us
  transfers between devices with their start and end apart: 4, of which 2 were waited for; matrix products, arithmetic and copies ran while one was open for 2% of the time, Pallas kernels for 0%

commit v1 on v0

v1 whole, which is shorter than its diff:
```python
import functools
import math

import jax
import jax.numpy as jnp
from jax import lax
from jax.experimental import pallas as pl
from jax.experimental.pallas import tpu as pltpu
from jax.sharding import PartitionSpec as P

BLK = 128
BACK = 7
NEVER = -4 * BLK


def from_behind(block, axis, distance):
    devices = range(lax.axis_size(axis))
    route = [(i - distance, i) for i in devices if i - distance in devices]
    return lax.ppermute(block, axis, route)


def attend_kernel(index_ref, bound_ref, q_ref, pool_ref, o_ref, score_ref, *, candidates, head_dim):
    block = pl.program_id(0)
    scale = 1.0 / math.sqrt(head_dim)
    queries = q_ref[...]
    row = lax.broadcasted_iota(jnp.int32, (BLK, BLK), 0)
    col = lax.broadcasted_iota(jnp.int32, (BLK, BLK), 1)
    offset = col - row
    running = None
    for k in range(candidates):
        slot = index_ref[block * candidates + k]
        bound = bound_ref[block * candidates + k]
        keys = pool_ref[slot, :, :head_dim]
        scores = (
            lax.dot_general(
                queries, keys, (((1,), (1,)), ((), ())), preferred_element_type=jnp.float32
            )
            * scale
        )
        scores = jnp.where(offset <= bound, scores, -1e30)
        score_ref[k] = scores
        running = scores if running is None else jnp.maximum(running, scores)
    row_max = jnp.max(running, axis=1, keepdims=True)
    total = None
    acc = None
    for k in range(candidates):
        slot = index_ref[block * candidates + k]
        bound = bound_ref[block * candidates + k]
        values = pool_ref[slot, :, head_dim:]
        weights = jnp.where(offset <= bound, jnp.exp(score_ref[k] - row_max), 0.0)
        total = weights if total is None else total + weights
        part = jnp.dot(weights.astype(jnp.bfloat16), values, preferred_element_type=jnp.float32)
        acc = part if acc is None else acc + part
    denominator = jnp.sum(total, axis=1, keepdims=True)
    o_ref[...] = (acc / denominator).astype(o_ref.dtype)


def attend(head_queries, key_pool, pool_index, bounds):
    range_len, head_dim = head_queries.shape
    blocks = range_len // BLK
    candidates = pool_index.shape[1]
    pool_size = key_pool.shape[0]
    kernel = functools.partial(attend_kernel, candidates=candidates, head_dim=head_dim)
    grid_spec = pltpu.PrefetchScalarGridSpec(
        num_scalar_prefetch=2,
        grid=(blocks,),
        in_specs=[
            pl.BlockSpec((BLK, head_dim), lambda i, *_: (i, 0)),
            pl.BlockSpec((pool_size, BLK, 2 * head_dim), lambda i, *_: (0, 0, 0)),
        ],
        out_specs=pl.BlockSpec((BLK, head_dim), lambda i, *_: (i, 0)),
        scratch_shapes=[pltpu.VMEM((candidates, BLK, BLK), jnp.float32)],
    )
    flops = 4 * range_len * candidates * BLK * head_dim
    return pl.pallas_call(
        kernel,
        grid_spec=grid_spec,
        out_shape=jax.ShapeDtypeStruct((range_len, head_dim), jnp.bfloat16),
        compiler_params=pltpu.CompilerParams(dimension_semantics=("arbitrary",)),
        cost_estimate=pl.CostEstimate(
            flops=flops,
            transcendentals=range_len * candidates * BLK,
            bytes_accessed=2 * range_len * head_dim * 2 + key_pool.size * 2,
        ),
    )(pool_index.reshape(-1), bounds.reshape(-1), head_queries, key_pool)


def shards(queries, keys, values, columns, offsets):
    tokens_dev = queries.shape[1]
    seq_count = lax.axis_size("seq")
    head_dim = queries.shape[2] // seq_count
    kv_heads = keys.shape[2] // head_dim
    group_size = seq_count // kv_heads
    vertical_count = columns.shape[1]
    local_queries = queries.reshape(tokens_dev, seq_count, head_dim)
    local_pairs = jnp.concatenate(
        [
            keys.reshape(tokens_dev, kv_heads, 1, head_dim),
            values.reshape(tokens_dev, kv_heads, 1, head_dim),
        ],
        axis=3,
    )
    local_pairs = jnp.broadcast_to(
        local_pairs, (tokens_dev, kv_heads, group_size, 2 * head_dim)
    ).reshape(tokens_dev, seq_count, 2 * head_dim)
    head_queries = lax.all_to_all(local_queries, "seq", split_axis=1, concat_axis=0, tiled=True)
    head_pairs = lax.all_to_all(local_pairs, "seq", split_axis=1, concat_axis=0, tiled=True)
    range_len = tokens_dev * seq_count
    blocks_slab = range_len // BLK
    head_queries = head_queries.reshape(range_len, head_dim)
    own_pairs = head_pairs.reshape(range_len, 2 * head_dim)
    own_blocks = own_pairs.reshape(blocks_slab, BLK, 2 * head_dim)
    head_index = lax.axis_index("seq")
    range_index = lax.axis_index("ctx")
    vertical = lax.dynamic_index_in_dim(columns, head_index, 0, keepdims=False)
    slashes = lax.dynamic_index_in_dim(offsets, head_index, 0, keepdims=False)
    first_block = range_index * blocks_slab
    local_index = vertical - first_block
    owned_mask = (local_index >= 0) & (local_index < blocks_slab)
    clipped_local = jnp.clip(local_index, 0, blocks_slab - 1)
    taken_blocks = own_blocks[clipped_local]
    slot_table = jnp.where(owned_mask[:, None, None], taken_blocks, jnp.zeros((), jnp.bfloat16))
    vertical_pairs = lax.psum(slot_table, "ctx")
    previous = from_behind(own_pairs[range_len - BACK * BLK :], "ctx", 1)
    key_pool = jnp.concatenate(
        [previous.reshape(BACK, BLK, 2 * head_dim), own_blocks, vertical_pairs], axis=0
    )
    pool_size = key_pool.shape[0]
    pool_base = first_block - BACK
    query_index = first_block + jnp.arange(blocks_slab, dtype=jnp.int32)
    slash_blocks = query_index[:, None] - slashes[None, :]
    repeated = jnp.any(slash_blocks[:, :, None] == vertical[None, None, :], axis=2)
    candidates = jnp.concatenate(
        [jnp.broadcast_to(vertical[None, :], (blocks_slab, vertical_count)), slash_blocks], axis=1
    )
    usable = jnp.concatenate(
        [jnp.ones((blocks_slab, vertical_count), dtype=bool), jnp.logical_not(repeated)], axis=1
    )
    usable = usable & (candidates >= 0) & (candidates <= query_index[:, None])
    strict = candidates < query_index[:, None]
    bounds = jnp.where(usable, jnp.where(strict, BLK, 0), NEVER).astype(jnp.int32)
    vertical_slots = jnp.broadcast_to(
        (BACK + blocks_slab + jnp.arange(vertical_count, dtype=jnp.int32))[None, :],
        (blocks_slab, vertical_count),
    )
    pool_index = jnp.concatenate([vertical_slots, slash_blocks - pool_base], axis=1)
    pool_index = jnp.clip(pool_index, 0, pool_size - 1).astype(jnp.int32)
    head_output = attend(head_queries, key_pool, pool_index, bounds).reshape(range_len, 1, head_dim)
    returned = lax.all_to_all(head_output, "seq", split_axis=0, concat_axis=1, tiled=True)
    return returned.reshape(1, tokens_dev, seq_count * head_dim)


def solution(mesh):
    placed = (P("ctx", "seq", None), P("ctx", "seq", None), P("ctx", "seq", None), P(), P())
    return jax.shard_map(
        shards, mesh=mesh, in_specs=placed, out_specs=P("ctx", "seq", None), check_vma=False
    )
```

time: 467 us -> 398 us (0.85)
  the two profiles are of different devices: /device:TPU:26 before, /device:TPU:24 now
where the time goes in v1:
time: 398 us
  waiting for transfers between devices  223 us (56%)
  blocking collectives  72.5 us (18%)
  Pallas kernels  35.7 us (9%)
  starting transfers between devices  30.3 us (8%)
  between operations  13.6 us (3%)
  local copies, waits for them, and re-layouts  12.4 us (3%)
  other arithmetic  10.3 us (3%)
    psum x1, waiting for transfers between devices, shards(): vertical_pairs = lax.psum(slot_table, 'ctx')  124 us
    all_to_all x1, waiting for transfers between devices, shards(): lax.all_to_all(local_pairs, 'seq', split_axis=1, concat_axis=0, tiled=True)  98.3 us
    all_to_all x1, blocking collectives, shards(): lax.all_to_all(head_output, 'seq', split_axis=0, concat_axis=1, tiled=True)  72.5 us
    pallas_call x1, Pallas kernels, attend(): pl.pallas_call(kernel, grid_spec=grid_spec, out_shape=jax.ShapeDtypeStruc...  35.7 us
    all_to_all x1, starting transfers between devices, shards(): lax.all_to_all(local_pairs, 'seq', split_axis=1, concat_axis=0, tiled=True)  22.2 us
  transfers between devices with their start and end apart: 4, of which 2 were waited for; matrix products, arithmetic and copies ran while one was open for 3% of the time, Pallas kernels for 0%

profile of v1, /device:TPU:24, one launch (start us, length us, event | category | flops | bytes accessed | tf_op | source)
XLA Modules:
  0.0 397.5 jit_solution(9416937172002323588)
XLA Ops:
  6.5 0.9 copy.31
  7.5 0.9 copy.32
  8.5 1.6 broadcast_in_dim.55
  10.1 22.2 %all-to-all-start.1 = ((bf16[64,64,256]{2,0,1:T(8,128)(2,1)}), bf16[64,64,256]{2,0,1:T(8,128)(2,1)S(1)}, u32[]{:S(2)}, u32[]{:S(2)}) async-start(bf16[64,64,256]{2,0,1:T(8,128)(2,1)} %bitcast.43), calls=%async_computation.1 | async-start | bytes 4194304 | tf_op jit(solution)/shard_map/all_to_all | solution.py:107
  32.7 1.7 copy.25
  34.3 98.3 %all-to-all-done.1 = bf16[64,64,256]{2,0,1:T(8,128)(2,1)S(1)} async-done(((bf16[64,64,256]{2,0,1:T(8,128)(2,1)}), bf16[64,64,256]{2,0,1:T(8,128)(2,1)S(1)}, u32[]{:S(2)}, u32[]{:S(2)}) %all-to-all-start.1) | async-done | bytes 2097184 | tf_op jit(solution)/shard_map/all_to_all | solution.py:107
  132.6 6.1 %all-to-all-start = ((bf16[64,64,128]{2,0,1:T(8,128)(2,1)}), bf16[64,64,128]{2,0,1:T(8,128)(2,1)}, u32[]{:S(2)}, u32[]{:S(2)}) async-start(bf16[64,64,128]{2,0,1:T(8,128)(2,1)} %copy.25), calls=%async_computation | async-start | bytes 2097152 | tf_op jit(solution)/shard_map/all_to_all | solution.py:106
  139.3 0.7 compare_reduce_fusion
  140.5 1.9 collective-permute-start
  143.1 1.5 broadcast_select_fusion
  144.6 0.6 pad.6.clone
  145.2 0.7 not.3
  145.9 0.8 add_clamp_fusion
  146.7 0.7 min.22.index_ref
  147.5 0.7 reshape.111.bound_ref
  148.2 124.5 %all-reduce.3.cloned.1.call-done = bf16[8,128,256]{2,1,0:T(8,128)(2,1)} async-done(((bf16[8,128,256]{2,1,0:T(8,128)(2,1)}), bf16[8,128,256]{2,1,0:T(8,128)(2,1)}) %all-reduce.3.cloned.1.call-update) | async-done | bytes 524304 | tf_op jit(solution)/shard_map/psum | solution.py:123
  272.7 3.1 pad_maximum_fusion.pool_ref
  275.7 35.7 %shard_map.55 = bf16[4096,128]{1,0:T(8,128)(2,1)} custom-call(s32[384]{0:T(512)} %min.22.index_ref, s32[384]{0:T(512)} %reshape.111.bound_ref, bf16[4096,128]{1,0:T(8,128)(2,1)} %bitcast.2.q_ref, bf16[47,128,256]{2,1,0:T(8,128)(2,1)} %pad_maximum_fusion.pool_ref), custom_call_target="tpu_custom_call" | custom-call | flops 3221225472 | bytes 5177344 | tf_op jit(solution)/shard_map/pallas_call | solution.py:75
  311.4 0.6 broadcast.124
  312.0 2.7 reduce.6
  315.0 72.5 %all_to_all.45 = bf16[64,2,4096]{2,1,0:T(2,128)(2,1)S(1)} all-to-all(bf16[64,2,4096]{2,1,0:T(2,128)(2,1)S(1)} %reshape.133), channel_id=1, replica_groups=mesh['seq'=64,'ctx'=16] {'seq'}, dimensions={0} | all-to-all | bytes 2097152 | tf_op jit(solution)/shard_map/all_to_all | solution.py:149
  387.5 1.0 reshape.134
  388.7 0.7 copy.28
  389.4 1.3 reshape.119
  (32 shorter events, 2.7 us)
Async XLA Ops:
  6.5 132.2 %copy-start = (s32[64,4]{0,1:T(4,128)S(1)}, s32[64,4]{0,1:T(4,128)}, u32[]{:S(2)}) copy-start(s32[64,4]{0,1:T(4,128)} %param.9) | copy-start | bytes 3076
  8.5 23.9 %copy-start.1 = (bf16[1,64,8192]{2,1,0:T(8,128)(2,1)S(1)}, bf16[1,64,8192]{2,1,0:T(8,128)(2,1)}, u32[]{:S(2)}) copy-start(bf16[1,64,8192]{2,1,0:T(8,128)(2,1)} %param.5) | copy-start | bytes 3145732
  10.1 122.5 %all-to-all-start.1 = ((bf16[64,64,256]{2,0,1:T(8,128)(2,1)}), bf16[64,64,256]{2,0,1:T(8,128)(2,1)S(1)}, u32[]{:S(2)}, u32[]{:S(2)}) async-start(bf16[64,64,256]{2,0,1:T(8,128)(2,1)} %bitcast.43), calls=%async_computation.1 | async-start | bytes 4194304 | tf_op jit(solution)/shard_map/all_to_all | solution.py:107
  32.4 106.6 %copy-start.2 = (s32[64,8]{0,1:T(8,128)S(1)}, s32[64,8]{0,1:T(8,128)}, u32[]{:S(2)}) copy-start(s32[64,8]{0,1:T(8,128)} %param.8) | copy-start | bytes 6148
  132.6 143.2 %all-to-all-start = ((bf16[64,64,128]{2,0,1:T(8,128)(2,1)}), bf16[64,64,128]{2,0,1:T(8,128)(2,1)}, u32[]{:S(2)}, u32[]{:S(2)}) async-start(bf16[64,64,128]{2,0,1:T(8,128)(2,1)} %copy.25), calls=%async_computation | async-start | bytes 2097152 | tf_op jit(solution)/shard_map/all_to_all | solution.py:106
  138.7 134.0 %all-reduce.3.cloned.1.call-start = ((), (), s32[]{:S(2)}) async-start(), calls=%async_computation.3 | async-start | bytes 1048576 | tf_op jit(solution)/shard_map/psum | solution.py:123
  139.2 1.3 copy-start.3
  139.2 1.3 copy-start.4
  140.5 132.2 %collective-permute-start = (bf16[896,256]{1,0:T(8,128)(2,1)S(1)}, bf16[896,256]{1,0:T(8,128)(2,1)S(1)}, u32[]{:S(2)}, u32[]{:S(2)}) collective-permute-start(bf16[896,256]{1,0:T(8,128)(2,1)S(1)} %bitcast.51), channel_id=1, source_target_pairs={{0,1},{1,2},{2,3},{3,4},{4,5},{5,6},{6,7},{7,8},{8,9},{9,10},{10,1... | collective-permute-start | bytes 1376264 | tf_op jit(solution)/shard_map/ppermute | solution.py:19
Sparse Core Ops, SparseCore 0:
  144.7 127.9 all-reduce.2

commit v2 on v1

--- a/solution.py
+++ b/solution.py
@@ -11,6 +11,7 @@
 BLK = 128
 BACK = 7
 NEVER = -4 * BLK
+VCAP = 2
 
 
 def from_behind(block, axis, distance):
@@ -115,12 +116,14 @@
     vertical = lax.dynamic_index_in_dim(columns, head_index, 0, keepdims=False)
     slashes = lax.dynamic_index_in_dim(offsets, head_index, 0, keepdims=False)
     first_block = range_index * blocks_slab
-    local_index = vertical - first_block
-    owned_mask = (local_index >= 0) & (local_index < blocks_slab)
-    clipped_local = jnp.clip(local_index, 0, blocks_slab - 1)
-    taken_blocks = own_blocks[clipped_local]
-    slot_table = jnp.where(owned_mask[:, None, None], taken_blocks, jnp.zeros((), jnp.bfloat16))
-    vertical_pairs = lax.psum(slot_table, "ctx")
+    owner = vertical // blocks_slab
+    earlier = jnp.arange(vertical_count)[None, :] < jnp.arange(vertical_count)[:, None]
+    rank = jnp.sum(earlier & (owner[None, :] == owner[:, None]), axis=1)
+    rank = jnp.clip(rank, 0, VCAP - 1)
+    held = (owner[None, :] == range_index) & (rank[None, :] == jnp.arange(VCAP)[:, None])
+    local_index = jnp.sum(jnp.where(held, vertical[None, :] - first_block, 0), axis=1)
+    taken_blocks = own_blocks[jnp.clip(local_index, 0, blocks_slab - 1)]
+    vertical_pairs = lax.all_gather(taken_blocks, "ctx", tiled=True)
     previous = from_behind(own_pairs[range_len - BACK * BLK :], "ctx", 1)
     key_pool = jnp.concatenate(
         [previous.reshape(BACK, BLK, 2 * head_dim), own_blocks, vertical_pairs], axis=0
@@ -140,7 +143,7 @@
     strict = candidates < query_index[:, None]
     bounds = jnp.where(usable, jnp.where(strict, BLK, 0), NEVER).astype(jnp.int32)
     vertical_slots = jnp.broadcast_to(
-        (BACK + blocks_slab + jnp.arange(vertical_count, dtype=jnp.int32))[None, :],
+        (BACK + blocks_slab + owner * VCAP + rank).astype(jnp.int32)[None, :],
         (blocks_slab, vertical_count),
     )
     pool_index = jnp.concatenate([vertical_slots, slash_blocks - pool_base], axis=1)

time: 398 us -> 307 us (0.77)
  the two profiles are of different devices: /device:TPU:24 before, /device:TPU:8 now
where the time goes in v2:
time: 307 us
  waiting for transfers between devices  146 us (48%)
  blocking collectives  59.8 us (19%)
  Pallas kernels  36.1 us (12%)
  starting transfers between devices  30.1 us (10%)
  local copies, waits for them, and re-layouts  14.3 us (5%)
  between operations  13.6 us (4%)
  other arithmetic  7 us (2%)
    all_to_all x1, waiting for transfers between devices, shards(): lax.all_to_all(local_pairs, 'seq', split_axis=1, concat_axis=0, tiled=True)  99.6 us
    all_to_all x1, blocking collectives, shards(): lax.all_to_all(head_output, 'seq', split_axis=0, concat_axis=1, tiled=True)  59.8 us
    pallas_call x1, Pallas kernels, attend(): pl.pallas_call(kernel, grid_spec=grid_spec, out_shape=jax.ShapeDtypeStruc...  36.1 us
    all_to_all x1, starting transfers between devices, shards(): lax.all_to_all(local_pairs, 'seq', split_axis=1, concat_axis=0, tiled=True)  22.4 us
    all_to_all x1, waiting for transfers between devices, shards(): lax.all_to_all(local_queries, 'seq', split_axis=1, concat_axis=0, tiled=T...  20.4 us
    all_gather x1, waiting for transfers between devices, shards(): vertical_pairs = lax.all_gather(taken_blocks, 'ctx', tiled=True)  16.4 us
    ppermute x1, waiting for transfers between devices, from_behind(): return lax.ppermute(block, axis, route)  9.53 us
  transfers between devices with their start and end apart: 4, of which 4 were waited for; matrix products, arithmetic and copies ran while one was open for 3% of the time, Pallas kernels for 0%

profile of v2, /device:TPU:8, one launch (start us, length us, event | category | flops | bytes accessed | tf_op | source)
XLA Modules:
  0.0 306.9 jit_solution(2243050447143822607)
XLA Ops:
  6.5 0.9 copy.38
  7.5 0.9 copy.39
  8.5 1.6 broadcast_in_dim.40
  10.1 22.4 %all-to-all-start.1 = ((bf16[64,64,256]{2,0,1:T(8,128)(2,1)}), bf16[64,64,256]{2,0,1:T(8,128)(2,1)S(1)}, u32[]{:S(2)}, u32[]{:S(2)}) async-start(bf16[64,64,256]{2,0,1:T(8,128)(2,1)} %bitcast.56), calls=%async_computation.1 | async-start | bytes 4194304 | tf_op jit(solution)/shard_map/all_to_all | solution.py:108
  33.1 99.6 %all-to-all-done.1 = bf16[64,64,256]{2,0,1:T(8,128)(2,1)S(1)} async-done(((bf16[64,64,256]{2,0,1:T(8,128)(2,1)}), bf16[64,64,256]{2,0,1:T(8,128)(2,1)S(1)}, u32[]{:S(2)}, u32[]{:S(2)}) %all-to-all-start.1) | async-done | bytes 2097184 | tf_op jit(solution)/shard_map/all_to_all | solution.py:108
  132.7 1.2 gather_fusion
  134.2 1.6 copy.31
  135.9 5.8 %all-to-all-start = ((bf16[64,64,128]{2,0,1:T(8,128)(2,1)}), bf16[64,64,128]{2,0,1:T(8,128)(2,1)S(1)}, u32[]{:S(2)}, u32[]{:S(2)}) async-start(bf16[64,64,128]{2,0,1:T(8,128)(2,1)} %copy.31), calls=%async_computation | async-start | bytes 2097152 | tf_op jit(solution)/shard_map/all_to_all | solution.py:107
  142.0 0.8 slice.10
  142.8 1.9 collective-permute-start
  145.0 0.7 min.32.index_ref
  145.8 0.7 reshape.131.bound_ref
  146.5 9.5 %collective-permute-done = bf16[896,256]{1,0:T(8,128)(2,1)} collective-permute-done((bf16[896,256]{1,0:T(8,128)(2,1)}, bf16[896,256]{1,0:T(8,128)(2,1)}, u32[]{:S(2)}, u32[]{:S(2)}) %collective-permute-start) | collective-permute-done | bytes 458784 | tf_op jit(solution)/shard_map/ppermute | solution.py:20
  156.1 16.4 %all-gather.3.cloned.1.call-done = bf16[32,128,256]{2,1,0:T(8,128)(2,1)} async-done(((bf16[2,128,256]{2,1,0:T(8,128)(2,1)}), bf16[32,128,256]{2,1,0:T(8,128)(2,1)}) %all-gather.3.cloned.1.call-update) | async-done | bytes 2097168 | tf_op jit(solution)/shard_map/all_gather | solution.py:126
  172.5 3.7 %pad_maximum_fusion.pool_ref = bf16[71,128,256]{2,1,0:T(8,128)(2,1)} fusion(bf16[32,128,256]{2,1,0:T(8,128)(2,1)} %all-gather.3.cloned.1.call-done, bf16[32,128,256]{2,1,0:T(8,128)(2,1)S(1)} %bitcast.55, bf16[7,128,256]{2,1,0:T(8,128)(2,1)} %bitcast.12), kind=kLoop, calls=%fused_computation.1 | loop fusion | flops 4653056 | bytes 9306112 | tf_op jit(solution)/shard_map/concatenate | solution.py:128
  176.1 20.4 %all-to-all-done = bf16[64,64,128]{2,0,1:T(8,128)(2,1)S(1)} async-done(((bf16[64,64,128]{2,0,1:T(8,128)(2,1)}), bf16[64,64,128]{2,0,1:T(8,128)(2,1)S(1)}, u32[]{:S(2)}, u32[]{:S(2)}) %all-to-all-start) | async-done | bytes 1048608 | tf_op jit(solution)/shard_map/all_to_all | solution.py:107
  196.5 1.0 copy-done.2
  197.5 36.1 %shard_map.55 = bf16[4096,128]{1,0:T(8,128)(2,1)} custom-call(s32[384]{0:T(512)} %min.32.index_ref, s32[384]{0:T(512)} %reshape.131.bound_ref, bf16[4096,128]{1,0:T(8,128)(2,1)} %bitcast.61, bf16[71,128,256]{2,1,0:T(8,128)(2,1)} %pad_maximum_fusion.pool_ref), custom_call_target="tpu_custom_call" | custom-call | flops 3221225472 | bytes 6750208 | tf_op jit(solution)/shard_map/pallas_call | solution.py:76
  233.6 0.5 broadcast.188
  234.1 2.7 reduce.2
  237.1 59.8 %all_to_all.45 = bf16[64,2,4096]{2,1,0:T(2,128)(2,1)S(1)} all-to-all(bf16[64,2,4096]{2,1,0:T(2,128)(2,1)S(1)} %reshape.152), channel_id=1, replica_groups=mesh['seq'=64,'ctx'=16] {'seq'}, dimensions={0} | all-to-all | bytes 2097152 | tf_op jit(solution)/shard_map/all_to_all | solution.py:152
  296.9 1.0 reshape.153
  298.1 0.7 copy.34
  298.8 1.3 reshape.139
  (35 shorter events, 2.0 us)
Async XLA Ops:
  6.5 26.0 %copy-start = (s32[64,8]{0,1:T(8,128)S(1)}, s32[64,8]{0,1:T(8,128)}, u32[]{:S(2)}) copy-start(s32[64,8]{0,1:T(8,128)} %param.8) | copy-start | bytes 6148
  10.1 123.8 %copy-start.1 = (bf16[1,64,8192]{2,1,0:T(8,128)(2,1)S(1)}, bf16[1,64,8192]{2,1,0:T(8,128)(2,1)}, u32[]{:S(2)}) copy-start(bf16[1,64,8192]{2,1,0:T(8,128)(2,1)} %param.5) | copy-start | bytes 3145732
  10.1 122.6 %all-to-all-start.1 = ((bf16[64,64,256]{2,0,1:T(8,128)(2,1)}), bf16[64,64,256]{2,0,1:T(8,128)(2,1)S(1)}, u32[]{:S(2)}, u32[]{:S(2)}) async-start(bf16[64,64,256]{2,0,1:T(8,128)(2,1)} %bitcast.56), calls=%async_computation.1 | async-start | bytes 4194304 | tf_op jit(solution)/shard_map/all_to_all | solution.py:108
  32.5 140.0 %all-gather.3.cloned.1.call-start = ((), (), s32[]{:S(2)}) async-start(), calls=%async_computation.3 | async-start | bytes 2228224 | tf_op jit(solution)/shard_map/all_gather | solution.py:126
  134.2 7.5 %copy-start.3 = (s32[64,4]{0,1:T(4,128)S(1)}, s32[64,4]{0,1:T(4,128)}, u32[]{:S(2)}) copy-start(s32[64,4]{0,1:T(4,128)} %param.9) | copy-start | bytes 3076
  135.9 60.6 %all-to-all-start = ((bf16[64,64,128]{2,0,1:T(8,128)(2,1)}), bf16[64,64,128]{2,0,1:T(8,128)(2,1)S(1)}, u32[]{:S(2)}, u32[]{:S(2)}) async-start(bf16[64,64,128]{2,0,1:T(8,128)(2,1)} %copy.31), calls=%async_computation | async-start | bytes 2097152 | tf_op jit(solution)/shard_map/all_to_all | solution.py:107
  142.8 13.3 %collective-permute-start = (bf16[896,256]{1,0:T(8,128)(2,1)}, bf16[896,256]{1,0:T(8,128)(2,1)}, u32[]{:S(2)}, u32[]{:S(2)}) collective-permute-start(bf16[896,256]{1,0:T(8,128)(2,1)} %bitcast.11), channel_id=1, source_target_pairs={{0,1},{1,2},{2,3},{3,4},{4,5},{5,6},{6,7},{7,8},{8,9},{9,10},{10,1... | collective-permute-start | bytes 1376264 | tf_op jit(solution)/shard_map/ppermute | solution.py:20
  196.5 1.0 copy-start.2
Sparse Core Ops, SparseCore 0:
  134.1 38.3 all-gather.2

commit v3 on v2

--- a/solution.py
+++ b/solution.py
@@ -6,9 +6,10 @@
 from jax import lax
 from jax.experimental import pallas as pl
 from jax.experimental.pallas import tpu as pltpu
-from jax.sharding import PartitionSpec as P
+from jax.sharding import Mesh, PartitionSpec as P
 
 BLK = 128
+SEQ = ("grp", "mem")
 BACK = 7
 NEVER = -4 * BLK
 VCAP = 2
@@ -88,30 +89,30 @@
 
 def shards(queries, keys, values, columns, offsets):
     tokens_dev = queries.shape[1]
-    seq_count = lax.axis_size("seq")
+    seq_count = lax.axis_size(SEQ)
     head_dim = queries.shape[2] // seq_count
     kv_heads = keys.shape[2] // head_dim
-    group_size = seq_count // kv_heads
     vertical_count = columns.shape[1]
     local_queries = queries.reshape(tokens_dev, seq_count, head_dim)
     local_pairs = jnp.concatenate(
         [
-            keys.reshape(tokens_dev, kv_heads, 1, head_dim),
-            values.reshape(tokens_dev, kv_heads, 1, head_dim),
+            keys.reshape(tokens_dev, kv_heads, head_dim),
+            values.reshape(tokens_dev, kv_heads, head_dim),
         ],
-        axis=3,
+        axis=2,
     )
-    local_pairs = jnp.broadcast_to(
-        local_pairs, (tokens_dev, kv_heads, group_size, 2 * head_dim)
-    ).reshape(tokens_dev, seq_count, 2 * head_dim)
-    head_queries = lax.all_to_all(local_queries, "seq", split_axis=1, concat_axis=0, tiled=True)
-    head_pairs = lax.all_to_all(local_pairs, "seq", split_axis=1, concat_axis=0, tiled=True)
+    group_pairs = lax.all_to_all(local_pairs, "grp", split_axis=1, concat_axis=0, tiled=True)
+    group_pairs = lax.all_gather(group_pairs, "mem", axis=0, tiled=False)
+    head_queries = lax.all_to_all(local_queries, SEQ, split_axis=1, concat_axis=0, tiled=True)
+    members = group_pairs.shape[0]
+    group_pairs = group_pairs.reshape(members, kv_heads, tokens_dev, 2 * head_dim)
+    head_pairs = jnp.transpose(group_pairs, (1, 0, 2, 3))
     range_len = tokens_dev * seq_count
     blocks_slab = range_len // BLK
     head_queries = head_queries.reshape(range_len, head_dim)
     own_pairs = head_pairs.reshape(range_len, 2 * head_dim)
     own_blocks = own_pairs.reshape(blocks_slab, BLK, 2 * head_dim)
-    head_index = lax.axis_index("seq")
+    head_index = lax.axis_index(SEQ)
     range_index = lax.axis_index("ctx")
     vertical = lax.dynamic_index_in_dim(columns, head_index, 0, keepdims=False)
     slashes = lax.dynamic_index_in_dim(offsets, head_index, 0, keepdims=False)
@@ -149,12 +150,24 @@
     pool_index = jnp.concatenate([vertical_slots, slash_blocks - pool_base], axis=1)
     pool_index = jnp.clip(pool_index, 0, pool_size - 1).astype(jnp.int32)
     head_output = attend(head_queries, key_pool, pool_index, bounds).reshape(range_len, 1, head_dim)
-    returned = lax.all_to_all(head_output, "seq", split_axis=0, concat_axis=1, tiled=True)
+    returned = lax.all_to_all(head_output, SEQ, split_axis=0, concat_axis=1, tiled=True)
     return returned.reshape(1, tokens_dev, seq_count * head_dim)
 
 
 def solution(mesh):
-    placed = (P("ctx", "seq", None), P("ctx", "seq", None), P("ctx", "seq", None), P(), P())
-    return jax.shard_map(
-        shards, mesh=mesh, in_specs=placed, out_specs=P("ctx", "seq", None), check_vma=False
-    )
+    def run(queries, keys, values, columns, offsets):
+        seq_count = mesh.shape["seq"]
+        kv_heads = keys.shape[2] // (queries.shape[2] // seq_count)
+        devices = mesh.devices.reshape(kv_heads, seq_count // kv_heads, mesh.shape["ctx"])
+        split = Mesh(devices, ("grp", "mem", "ctx"))
+        placed = P("ctx", SEQ, None)
+        step = jax.shard_map(
+            shards,
+            mesh=split,
+            in_specs=(placed, placed, placed, P(), P()),
+            out_specs=placed,
+            check_vma=False,
+        )
+        return step(queries, keys, values, columns, offsets)
+
+    return run

time: 307 us -> 271 us (0.88)
  the two profiles are of different devices: /device:TPU:8 before, /device:TPU:2 now
where the time goes in v3:
time: 271 us
  blocking collectives  96 us (35%)
  waiting for transfers between devices  85.3 us (31%)
  Pallas kernels  36.1 us (13%)
  starting transfers between devices  18.3 us (7%)
  local copies, waits for them, and re-layouts  14.5 us (5%)
  between operations  13.6 us (5%)
  other arithmetic  6.93 us (3%)
    all_to_all x1, blocking collectives, shards(): lax.all_to_all(head_output, SEQ, split_axis=0, concat_axis=1, tiled=True)  57.8 us
    all_gather x1, waiting for transfers between devices, shards(): group_pairs = lax.all_gather(group_pairs, 'mem', axis=0, tiled=False)  43.4 us
    all_to_all x1, blocking collectives, shards(): lax.all_to_all(local_pairs, 'grp', split_axis=1, concat_axis=0, tiled=True)  38.1 us
    pallas_call x1, Pallas kernels, attend(): pl.pallas_call(kernel, grid_spec=grid_spec, out_shape=jax.ShapeDtypeStruc...  36.1 us
    all_gather x1, waiting for transfers between devices, shards(): vertical_pairs = lax.all_gather(taken_blocks, 'ctx', tiled=True)  25.6 us
    all_to_all x1, waiting for transfers between devices, shards(): lax.all_to_all(local_queries, SEQ, split_axis=1, concat_axis=0, tiled=True)  16.2 us
    all_to_all x1, starting transfers between devices, shards(): lax.all_to_all(local_queries, SEQ, split_axis=1, concat_axis=0, tiled=True)  16.2 us
  transfers between devices with their start and end apart: 4, of which 3 were waited for; matrix products, arithmetic and copies ran while one was open for 3% of the time, Pallas kernels for 0%

profile of v3, /device:TPU:2, one launch (start us, length us, event | category | flops | bytes accessed | tf_op | source)
XLA Modules:
  0.0 270.7 jit_solution(4448494493608177271)
XLA Ops:
  6.5 0.9 copy.51
  7.5 0.9 copy.52
  8.5 38.1 %all_to_all.45 = bf16[64,8,256]{2,0,1:T(8,128)(2,1)} all-to-all(bf16[64,8,256]{2,0,1:T(8,128)(2,1)S(1)} %copy.43), channel_id=1, replica_groups=mesh['grp'=8,'mem'=8,'ctx'=16] {'grp'}, dimensions={1} | all-to-all | bytes 524288 | tf_op jit(solution)/shard_map/all_to_all | solution.py:104
  47.3 43.4 %all-gather.4.cloned.1.call-done = bf16[8,512,1,256]{3,1,2,0:T(8,128)(2,1)} async-done(((bf16[1,512,1,256]{3,1,2,0:T(8,128)(2,1)}), bf16[8,512,1,256]{3,1,2,0:T(8,128)(2,1)}) %all-gather.4.cloned.1.call-update) | async-done | bytes 2097168 | tf_op jit(solution)/shard_map/all_gather | solution.py:105
  90.7 1.8 copy.44
  92.5 1.2 gather_fusion
  94.0 1.6 copy.42
  95.7 16.2 %all-to-all-start = ((bf16[64,64,128]{2,0,1:T(8,128)(2,1)}), bf16[64,64,128]{2,0,1:T(8,128)(2,1)S(1)}, u32[]{:S(2)}, u32[]{:S(2)}) async-start(bf16[64,64,128]{2,0,1:T(8,128)(2,1)} %copy.42), calls=%async_computation | async-start | bytes 2097152 | tf_op jit(solution)/shard_map/all_to_all | solution.py:106
  112.1 0.8 slice.6
  112.9 2.1 collective-permute-start
  115.3 0.7 min.32.index_ref
  116.1 0.7 reshape.131.bound_ref
  116.8 25.6 %all-gather.6.cloned.1.call-done = bf16[32,128,256]{2,1,0:T(8,128)(2,1)} async-done(((bf16[2,128,256]{2,1,0:T(8,128)(2,1)}), bf16[32,128,256]{2,1,0:T(8,128)(2,1)}) %all-gather.6.cloned.1.call-update) | async-done | bytes 2097168 | tf_op jit(solution)/shard_map/all_gather | solution.py:127
  142.4 3.6 %pad_maximum_fusion.pool_ref = bf16[71,128,256]{2,1,0:T(8,128)(2,1)} fusion(bf16[32,128,256]{2,1,0:T(8,128)(2,1)} %all-gather.6.cloned.1.call-done, bf16[32,128,256]{2,1,0:T(8,128)(2,1)S(1)} %bitcast.52, bf16[7,128,256]{2,1,0:T(8,128)(2,1)} %bitcast.13), kind=kLoop, calls=%fused_computation.1 | loop fusion | flops 4653056 | bytes 9306112 | tf_op jit(solution)/shard_map/concatenate | solution.py:129
  146.0 16.2 %all-to-all-done = bf16[64,64,128]{2,0,1:T(8,128)(2,1)S(1)} async-done(((bf16[64,64,128]{2,0,1:T(8,128)(2,1)}), bf16[64,64,128]{2,0,1:T(8,128)(2,1)S(1)}, u32[]{:S(2)}, u32[]{:S(2)}) %all-to-all-start) | async-done | bytes 1048608 | tf_op jit(solution)/shard_map/all_to_all | solution.py:106
  162.3 1.0 copy-done.2
  163.2 36.1 %shard_map.55 = bf16[4096,128]{1,0:T(8,128)(2,1)} custom-call(s32[384]{0:T(512)} %min.32.index_ref, s32[384]{0:T(512)} %reshape.131.bound_ref, bf16[4096,128]{1,0:T(8,128)(2,1)} %bitcast.58, bf16[71,128,256]{2,1,0:T(8,128)(2,1)} %pad_maximum_fusion.pool_ref), custom_call_target="tpu_custom_call" | custom-call | flops 3221225472 | bytes 6750208 | tf_op jit(solution)/shard_map/pallas_call | solution.py:77
  199.3 0.5 broadcast.188
  199.9 2.7 reduce.2
  202.5 0.3 reshape.153
  202.8 57.8 %all_to_all.46 = bf16[64,2,4096]{2,1,0:T(2,128)(2,1)S(1)} all-to-all(bf16[64,2,4096]{2,1,0:T(2,128)(2,1)S(1)} %reshape.153), channel_id=1, replica_groups=mesh['grp'=8,'mem'=8,'ctx'=16] {'grp','mem'}, dimensions={0} | all-to-all | bytes 2097152 | tf_op jit(solution)/shard_map/all_to_all | solution.py:153
  260.7 1.0 reshape.154
  261.9 0.7 copy.47
  262.5 1.3 reshape.140
  (37 shorter events, 1.7 us)
Async XLA Ops:
  6.5 40.2 %copy-start = (s32[64,8]{0,1:T(8,128)S(1)}, s32[64,8]{0,1:T(8,128)}, u32[]{:S(2)}) copy-start(s32[64,8]{0,1:T(8,128)} %param.8) | copy-start | bytes 6148
  6.5 84.1 %all-gather.4.cloned.1.call-start = ((), (), s32[]{:S(2)}) async-start(), calls=%async_computation.3 | async-start | bytes 2359296 | tf_op jit(solution)/shard_map/all_gather | solution.py:105
  46.7 95.7 %all-gather.6.cloned.1.call-start = ((), (), s32[]{:S(2)}) async-start(), calls=%async_computation.4 | async-start | bytes 2228224 | tf_op jit(solution)/shard_map/all_gather | solution.py:127
  90.7 3.1 %copy-start.1 = (bf16[1,64,8192]{2,1,0:T(8,128)(2,1)S(1)}, bf16[1,64,8192]{2,1,0:T(8,128)(2,1)}, u32[]{:S(2)}) copy-start(bf16[1,64,8192]{2,1,0:T(8,128)(2,1)} %param.5) | copy-start | bytes 3145732
  94.0 17.9 %copy-start.3 = (s32[64,4]{0,1:T(4,128)S(1)}, s32[64,4]{0,1:T(4,128)}, u32[]{:S(2)}) copy-start(s32[64,4]{0,1:T(4,128)} %param.9) | copy-start | bytes 3076
  95.7 66.6 %all-to-all-start = ((bf16[64,64,128]{2,0,1:T(8,128)(2,1)}), bf16[64,64,128]{2,0,1:T(8,128)(2,1)S(1)}, u32[]{:S(2)}, u32[]{:S(2)}) async-start(bf16[64,64,128]{2,0,1:T(8,128)(2,1)} %copy.42), calls=%async_computation | async-start | bytes 2097152 | tf_op jit(solution)/shard_map/all_to_all | solution.py:106
  112.9 3.9 %collective-permute-start = (bf16[896,256]{1,0:T(8,128)(2,1)}, bf16[896,256]{1,0:T(8,128)(2,1)}, u32[]{:S(2)}, u32[]{:S(2)}) collective-permute-start(bf16[896,256]{1,0:T(8,128)(2,1)} %slice.6), channel_id=1, source_target_pairs={{0,1},{1,2},{2,3},{3,4},{4,5},{5,6},{6,7},{7,8},{8,9},{9,10},{10,1... | collective-permute-start | bytes 1376264 | tf_op jit(solution)/shard_map/ppermute | solution.py:21
  162.3 1.0 copy-start.2
Sparse Core Ops, SparseCore 0:
  46.8 43.8 all-gather.3
  93.8 48.4 all-gather.5

commit v4 on v3

--- a/solution.py
+++ b/solution.py
@@ -21,57 +21,62 @@
     return lax.ppermute(block, axis, route)
 
 
-def attend_kernel(index_ref, bound_ref, q_ref, pool_ref, o_ref, score_ref, *, candidates, head_dim):
-    block = pl.program_id(0)
+def attend_kernel(
+    index_ref, bound_ref, q_ref, pool_ref, o_ref, key_ref, value_ref, *, candidates, head_dim, per_step
+):
+    step = pl.program_id(0)
     scale = 1.0 / math.sqrt(head_dim)
-    queries = q_ref[...]
     row = lax.broadcasted_iota(jnp.int32, (BLK, BLK), 0)
     col = lax.broadcasted_iota(jnp.int32, (BLK, BLK), 1)
     offset = col - row
-    running = None
-    for k in range(candidates):
-        slot = index_ref[block * candidates + k]
-        bound = bound_ref[block * candidates + k]
-        keys = pool_ref[slot, :, :head_dim]
+    for part in range(per_step):
+        block = step * per_step + part
+        for k in range(candidates):
+            slot = index_ref[block * candidates + k]
+            key_ref[k * BLK : (k + 1) * BLK, :] = pool_ref[slot, :, :head_dim]
+            value_ref[k * BLK : (k + 1) * BLK, :] = pool_ref[slot, :, head_dim:]
+        queries = q_ref[part * BLK : (part + 1) * BLK, :]
         scores = (
             lax.dot_general(
-                queries, keys, (((1,), (1,)), ((), ())), preferred_element_type=jnp.float32
+                queries, key_ref[...], (((1,), (1,)), ((), ())), preferred_element_type=jnp.float32
             )
             * scale
         )
-        scores = jnp.where(offset <= bound, scores, -1e30)
-        score_ref[k] = scores
-        running = scores if running is None else jnp.maximum(running, scores)
-    row_max = jnp.max(running, axis=1, keepdims=True)
-    total = None
-    acc = None
-    for k in range(candidates):
-        slot = index_ref[block * candidates + k]
-        bound = bound_ref[block * candidates + k]
-        values = pool_ref[slot, :, head_dim:]
-        weights = jnp.where(offset <= bound, jnp.exp(score_ref[k] - row_max), 0.0)
-        total = weights if total is None else total + weights
-        part = jnp.dot(weights.astype(jnp.bfloat16), values, preferred_element_type=jnp.float32)
-        acc = part if acc is None else acc + part
-    denominator = jnp.sum(total, axis=1, keepdims=True)
-    o_ref[...] = (acc / denominator).astype(o_ref.dtype)
+        masked = []
+        for k in range(candidates):
+            bound = bound_ref[block * candidates + k]
+            masked.append(jnp.where(offset <= bound, scores[:, k * BLK : (k + 1) * BLK], -1e30))
+        scores = jnp.concatenate(masked, axis=1)
+        row_max = jnp.max(scores, axis=1, keepdims=True)
+        weights = jnp.exp(scores - row_max)
+        denominator = jnp.sum(weights, axis=1, keepdims=True)
+        weighted = jnp.dot(
+            weights.astype(jnp.bfloat16), value_ref[...], preferred_element_type=jnp.float32
+        )
+        o_ref[part * BLK : (part + 1) * BLK, :] = (weighted / denominator).astype(o_ref.dtype)
 
 
-def attend(head_queries, key_pool, pool_index, bounds):
+def attend(head_queries, key_pool, pool_index, bounds, per_step=2):
     range_len, head_dim = head_queries.shape
     blocks = range_len // BLK
     candidates = pool_index.shape[1]
     pool_size = key_pool.shape[0]
-    kernel = functools.partial(attend_kernel, candidates=candidates, head_dim=head_dim)
+    kernel = functools.partial(
+        attend_kernel, candidates=candidates, head_dim=head_dim, per_step=per_step
+    )
+    rows = per_step * BLK
     grid_spec = pltpu.PrefetchScalarGridSpec(
         num_scalar_prefetch=2,
-        grid=(blocks,),
+        grid=(blocks // per_step,),
         in_specs=[
-            pl.BlockSpec((BLK, head_dim), lambda i, *_: (i, 0)),
+            pl.BlockSpec((rows, head_dim), lambda i, *_: (i, 0)),
             pl.BlockSpec((pool_size, BLK, 2 * head_dim), lambda i, *_: (0, 0, 0)),
         ],
-        out_specs=pl.BlockSpec((BLK, head_dim), lambda i, *_: (i, 0)),
-        scratch_shapes=[pltpu.VMEM((candidates, BLK, BLK), jnp.float32)],
+        out_specs=pl.BlockSpec((rows, head_dim), lambda i, *_: (i, 0)),
+        scratch_shapes=[
+            pltpu.VMEM((candidates * BLK, head_dim), jnp.bfloat16),
+            pltpu.VMEM((candidates * BLK, head_dim), jnp.bfloat16),
+        ],
     )
     flops = 4 * range_len * candidates * BLK * head_dim
     return pl.pallas_call(

time: 271 us -> 260 us (0.959)
  Pallas kernels: 36.1 us -> 24.6 us
    pallas_call x1, Pallas kernels: 36.1 us -> 24.6 us  [attend(): pl.pallas_call(kernel, grid_spec=grid_spec, out_shape=jax.ShapeDtypeStruc...]
where the time goes in v4:
time: 260 us; the launch traced here: 259 us
  blocking collectives  96 us (37%)
  waiting for transfers between devices  85.3 us (33%)
  Pallas kernels  24.6 us (9%)
  starting transfers between devices  18.3 us (7%)
  local copies, waits for them, and re-layouts  14.5 us (6%)
  between operations  13.6 us (5%)
  other arithmetic  6.93 us (3%)
    all_to_all x1, blocking collectives, shards(): lax.all_to_all(head_output, SEQ, split_axis=0, concat_axis=1, tiled=True)  57.8 us
    all_gather x1, waiting for transfers between devices, shards(): group_pairs = lax.all_gather(group_pairs, 'mem', axis=0, tiled=False)  43.4 us
    all_to_all x1, blocking collectives, shards(): lax.all_to_all(local_pairs, 'grp', split_axis=1, concat_axis=0, tiled=True)  38.1 us
    all_gather x1, waiting for transfers between devices, shards(): vertical_pairs = lax.all_gather(taken_blocks, 'ctx', tiled=True)  25.6 us
    pallas_call x1, Pallas kernels, attend(): pl.pallas_call(kernel, grid_spec=grid_spec, out_shape=jax.ShapeDtypeStruc...  24.6 us
    all_to_all x1, waiting for transfers between devices, shards(): lax.all_to_all(local_queries, SEQ, split_axis=1, concat_axis=0, tiled=True)  16.2 us
    all_to_all x1, starting transfers between devices, shards(): lax.all_to_all(local_queries, SEQ, split_axis=1, concat_axis=0, tiled=True)  16.2 us
  transfers between devices with their start and end apart: 4, of which 3 were waited for; matrix products, arithmetic and copies ran while one was open for 3% of the time, Pallas kernels for 0%

profile of v4, /device:TPU:2, one launch (start us, length us, event | category | flops | bytes accessed | tf_op | source)
XLA Modules:
  0.0 259.2 jit_solution(12613008680647968386)
XLA Ops:
  6.5 0.9 copy.51
  7.5 0.9 copy.52
  8.5 38.1 %all_to_all.45 = bf16[64,8,256]{2,0,1:T(8,128)(2,1)} all-to-all(bf16[64,8,256]{2,0,1:T(8,128)(2,1)S(1)} %copy.43), channel_id=1, replica_groups=mesh['grp'=8,'mem'=8,'ctx'=16] {'grp'}, dimensions={1} | all-to-all | bytes 524288 | tf_op jit(solution)/shard_map/all_to_all | solution.py:109
  47.3 43.4 %all-gather.4.cloned.1.call-done = bf16[8,512,1,256]{3,1,2,0:T(8,128)(2,1)} async-done(((bf16[1,512,1,256]{3,1,2,0:T(8,128)(2,1)}), bf16[8,512,1,256]{3,1,2,0:T(8,128)(2,1)}) %all-gather.4.cloned.1.call-update) | async-done | bytes 2097168 | tf_op jit(solution)/shard_map/all_gather | solution.py:110
  90.7 1.8 copy.44
  92.5 1.2 gather_fusion
  94.0 1.6 copy.42
  95.7 16.2 %all-to-all-start = ((bf16[64,64,128]{2,0,1:T(8,128)(2,1)}), bf16[64,64,128]{2,0,1:T(8,128)(2,1)S(1)}, u32[]{:S(2)}, u32[]{:S(2)}) async-start(bf16[64,64,128]{2,0,1:T(8,128)(2,1)} %copy.42), calls=%async_computation | async-start | bytes 2097152 | tf_op jit(solution)/shard_map/all_to_all | solution.py:111
  112.1 0.8 slice.6
  112.9 2.1 collective-permute-start
  115.3 0.7 min.32.index_ref
  116.1 0.7 reshape.131.bound_ref
  116.8 25.6 %all-gather.6.cloned.1.call-done = bf16[32,128,256]{2,1,0:T(8,128)(2,1)} async-done(((bf16[2,128,256]{2,1,0:T(8,128)(2,1)}), bf16[32,128,256]{2,1,0:T(8,128)(2,1)}) %all-gather.6.cloned.1.call-update) | async-done | bytes 2097168 | tf_op jit(solution)/shard_map/all_gather | solution.py:132
  142.4 3.6 %pad_maximum_fusion.pool_ref = bf16[71,128,256]{2,1,0:T(8,128)(2,1)} fusion(bf16[32,128,256]{2,1,0:T(8,128)(2,1)} %all-gather.6.cloned.1.call-done, bf16[32,128,256]{2,1,0:T(8,128)(2,1)S(1)} %bitcast.52, bf16[7,128,256]{2,1,0:T(8,128)(2,1)} %bitcast.13), kind=kLoop, calls=%fused_computation.1 | loop fusion | flops 4653056 | bytes 9306112 | tf_op jit(solution)/shard_map/concatenate | solution.py:134
  146.0 16.2 %all-to-all-done = bf16[64,64,128]{2,0,1:T(8,128)(2,1)S(1)} async-done(((bf16[64,64,128]{2,0,1:T(8,128)(2,1)}), bf16[64,64,128]{2,0,1:T(8,128)(2,1)S(1)}, u32[]{:S(2)}, u32[]{:S(2)}) %all-to-all-start) | async-done | bytes 1048608 | tf_op jit(solution)/shard_map/all_to_all | solution.py:111
  162.3 1.0 copy-done.2
  163.2 24.6 %shard_map.55 = bf16[4096,128]{1,0:T(8,128)(2,1)} custom-call(s32[384]{0:T(512)} %min.32.index_ref, s32[384]{0:T(512)} %reshape.131.bound_ref, bf16[4096,128]{1,0:T(8,128)(2,1)} %bitcast.58, bf16[71,128,256]{2,1,0:T(8,128)(2,1)} %pad_maximum_fusion.pool_ref), custom_call_target="tpu_custom_call" | custom-call | flops 3221225472 | bytes 6750208 | tf_op jit(solution)/shard_map/pallas_call | solution.py:82
  187.9 0.5 broadcast.188
  188.4 2.7 %reduce.2 = bf16[4096,128]{1,0:T(8,128)(2,1)S(1)} reduce(bf16[4096,1,128]{2,0,1:T(8,128)(2,1)} %bitcast.56, bf16[]{:T(256)} %broadcast.188), dimensions={1}, to_apply=%copy.46.reduce_sub_computation | reduce | bytes 2097154 | tf_op jit(solution)/shard_map/reshape | solution.py:157
  191.1 0.3 reshape.153
  191.3 57.8 %all_to_all.46 = bf16[64,2,4096]{2,1,0:T(2,128)(2,1)S(1)} all-to-all(bf16[64,2,4096]{2,1,0:T(2,128)(2,1)S(1)} %reshape.153), channel_id=1, replica_groups=mesh['grp'=8,'mem'=8,'ctx'=16] {'grp','mem'}, dimensions={0} | all-to-all | bytes 2097152 | tf_op jit(solution)/shard_map/all_to_all | solution.py:158
  249.2 1.0 reshape.154
  250.4 0.7 copy.47
  251.1 1.3 reshape.140
  (37 shorter events, 1.7 us)
Async XLA Ops:
  6.5 40.2 %copy-start = (s32[64,8]{0,1:T(8,128)S(1)}, s32[64,8]{0,1:T(8,128)}, u32[]{:S(2)}) copy-start(s32[64,8]{0,1:T(8,128)} %param.8) | copy-start | bytes 6148
  6.5 84.1 %all-gather.4.cloned.1.call-start = ((), (), s32[]{:S(2)}) async-start(), calls=%async_computation.3 | async-start | bytes 2359296 | tf_op jit(solution)/shard_map/all_gather | solution.py:110
  46.7 95.7 %all-gather.6.cloned.1.call-start = ((), (), s32[]{:S(2)}) async-start(), calls=%async_computation.4 | async-start | bytes 2228224 | tf_op jit(solution)/shard_map/all_gather | solution.py:132
  90.7 3.1 %copy-start.1 = (bf16[1,64,8192]{2,1,0:T(8,128)(2,1)S(1)}, bf16[1,64,8192]{2,1,0:T(8,128)(2,1)}, u32[]{:S(2)}) copy-start(bf16[1,64,8192]{2,1,0:T(8,128)(2,1)} %param.5) | copy-start | bytes 3145732
  94.0 17.9 %copy-start.3 = (s32[64,4]{0,1:T(4,128)S(1)}, s32[64,4]{0,1:T(4,128)}, u32[]{:S(2)}) copy-start(s32[64,4]{0,1:T(4,128)} %param.9) | copy-start | bytes 3076
  95.7 66.6 %all-to-all-start = ((bf16[64,64,128]{2,0,1:T(8,128)(2,1)}), bf16[64,64,128]{2,0,1:T(8,128)(2,1)S(1)}, u32[]{:S(2)}, u32[]{:S(2)}) async-start(bf16[64,64,128]{2,0,1:T(8,128)(2,1)} %copy.42), calls=%async_computation | async-start | bytes 2097152 | tf_op jit(solution)/shard_map/all_to_all | solution.py:111
  112.9 3.9 %collective-permute-start = (bf16[896,256]{1,0:T(8,128)(2,1)}, bf16[896,256]{1,0:T(8,128)(2,1)}, u32[]{:S(2)}, u32[]{:S(2)}) collective-permute-start(bf16[896,256]{1,0:T(8,128)(2,1)} %slice.6), channel_id=1, source_target_pairs={{0,1},{1,2},{2,3},{3,4},{4,5},{5,6},{6,7},{7,8},{8,9},{9,10},{10,1... | collective-permute-start | bytes 1376264 | tf_op jit(solution)/shard_map/ppermute | solution.py:21
  162.3 1.0 copy-start.2
Sparse Core Ops, SparseCore 0:
  46.8 43.8 all-gather.3
  93.8 48.4 all-gather.5

commit v5 on v4

--- a/solution.py
+++ b/solution.py
@@ -107,9 +107,10 @@
         axis=2,
     )
     group_pairs = lax.all_to_all(local_pairs, "grp", split_axis=1, concat_axis=0, tiled=True)
-    group_pairs = lax.all_gather(group_pairs, "mem", axis=0, tiled=False)
+    members = lax.axis_size("mem")
+    group_pairs = jnp.broadcast_to(group_pairs[None], (members,) + group_pairs.shape)
+    group_pairs = lax.all_to_all(group_pairs, "mem", split_axis=0, concat_axis=0, tiled=True)
     head_queries = lax.all_to_all(local_queries, SEQ, split_axis=1, concat_axis=0, tiled=True)
-    members = group_pairs.shape[0]
     group_pairs = group_pairs.reshape(members, kv_heads, tokens_dev, 2 * head_dim)
     head_pairs = jnp.transpose(group_pairs, (1, 0, 2, 3))
     range_len = tokens_dev * seq_count

time: 260 us -> 247 us (0.950)
  the two profiles are of different devices: /device:TPU:2 before, /device:TPU:48 now
where the time goes in v5:
time: 247 us
  blocking collectives  98.1 us (40%)
  waiting for transfers between devices  70 us (28%)
  Pallas kernels  24.7 us (10%)
  local copies, waits for them, and re-layouts  17.4 us (7%)
  starting transfers between devices  16.1 us (7%)
  between operations  13.6 us (6%)
  other arithmetic  6.94 us (3%)
    all_to_all x1, blocking collectives, shards(): lax.all_to_all(head_output, SEQ, split_axis=0, concat_axis=1, tiled=True)  60 us
    all_to_all x1, blocking collectives, shards(): lax.all_to_all(local_pairs, 'grp', split_axis=1, concat_axis=0, tiled=True)  38 us
    pallas_call x1, Pallas kernels, attend(): pl.pallas_call(kernel, grid_spec=grid_spec, out_shape=jax.ShapeDtypeStruc...  24.7 us
    all_to_all x1, waiting for transfers between devices, shards(): lax.all_to_all(group_pairs, 'mem', split_axis=0, concat_axis=0, tiled=True)  23.3 us
    all_to_all x1, waiting for transfers between devices, shards(): lax.all_to_all(local_queries, SEQ, split_axis=1, concat_axis=0, tiled=True)  22.9 us
    all_gather x1, waiting for transfers between devices, shards(): vertical_pairs = lax.all_gather(taken_blocks, 'ctx', tiled=True)  13.7 us
    ppermute x1, waiting for transfers between devices, from_behind(): return lax.ppermute(block, axis, route)  10 us
    all_to_all x1, starting transfers between devices, shards(): lax.all_to_all(local_queries, SEQ, split_axis=1, concat_axis=0, tiled=True)  8.29 us
  transfers between devices with their start and end apart: 4, of which 4 were waited for; matrix products, arithmetic and copies ran while one was open for 4% of the time, Pallas kernels for 0%

profile of v5, /device:TPU:48, one launch (start us, length us, event | category | flops | bytes accessed | tf_op | source)
XLA Modules:
  0.0 246.7 jit_solution(9952188625056121143)
XLA Ops:
  6.5 0.9 copy.51
  7.5 0.9 copy.52
  8.5 38.0 %all_to_all.50 = bf16[64,8,256]{2,0,1:T(8,128)(2,1)S(1)} all-to-all(bf16[64,8,256]{2,0,1:T(8,128)(2,1)S(1)} %copy.43), channel_id=1, replica_groups=mesh['grp'=8,'mem'=8,'ctx'=16] {'grp'}, dimensions={1} | all-to-all | bytes 524288 | tf_op jit(solution)/shard_map/all_to_all | solution.py:109
  46.5 1.5 broadcast_in_dim.40
  48.0 5.9 %all-to-all-start.2 = ((bf16[8,512,1,256]{3,1,2,0:T(8,128)(2,1)}), bf16[8,512,1,256]{3,1,2,0:T(8,128)(2,1)S(1)}, u32[]{:S(2)}, u32[]{:S(2)}) async-start(bf16[8,512,1,256]{3,1,2,0:T(8,128)(2,1)} %broadcast_in_dim.40), calls=%async_computation.2 | async-start | bytes 4194304 | tf_op jit(solution)/shard_map/all_to_all | solution.py:112
  54.5 23.3 %all-to-all-done.2 = bf16[8,512,1,256]{3,1,2,0:T(8,128)(2,1)S(1)} async-done(((bf16[8,512,1,256]{3,1,2,0:T(8,128)(2,1)}), bf16[8,512,1,256]{3,1,2,0:T(8,128)(2,1)S(1)}, u32[]{:S(2)}, u32[]{:S(2)}) %all-to-all-start.2) | async-done | bytes 2097184 | tf_op jit(solution)/shard_map/all_to_all | solution.py:112
  77.8 1.3 copy-done.1
  79.1 1.9 copy.44
  81.1 1.2 gather_fusion
  82.6 1.6 copy.42
  84.2 8.3 %all-to-all-start = ((bf16[64,64,128]{2,0,1:T(8,128)(2,1)}), bf16[64,64,128]{2,0,1:T(8,128)(2,1)S(1)}, u32[]{:S(2)}, u32[]{:S(2)}) async-start(bf16[64,64,128]{2,0,1:T(8,128)(2,1)} %copy.42), calls=%async_computation | async-start | bytes 2097152 | tf_op jit(solution)/shard_map/all_to_all | solution.py:113
  92.8 0.8 slice.6
  93.6 1.9 collective-permute-start
  96.6 0.7 reshape.134.bound_ref
  97.3 10.0 %collective-permute-done = bf16[896,256]{1,0:T(8,128)(2,1)} collective-permute-done((bf16[896,256]{1,0:T(8,128)(2,1)}, bf16[896,256]{1,0:T(8,128)(2,1)}, u32[]{:S(2)}, u32[]{:S(2)}) %collective-permute-start) | collective-permute-done | bytes 458784 | tf_op jit(solution)/shard_map/ppermute | solution.py:21
  107.4 13.7 %all-gather.3.cloned.1.call-done = bf16[32,128,256]{2,1,0:T(8,128)(2,1)} async-done(((bf16[2,128,256]{2,1,0:T(8,128)(2,1)}), bf16[32,128,256]{2,1,0:T(8,128)(2,1)}) %all-gather.3.cloned.1.call-update) | async-done | bytes 2097168 | tf_op jit(solution)/shard_map/all_gather | solution.py:133
  121.1 3.6 %pad_maximum_fusion.pool_ref = bf16[71,128,256]{2,1,0:T(8,128)(2,1)} fusion(bf16[32,128,256]{2,1,0:T(8,128)(2,1)} %all-gather.3.cloned.1.call-done, bf16[32,128,256]{2,1,0:T(8,128)(2,1)S(1)} %bitcast.52, bf16[7,128,256]{2,1,0:T(8,128)(2,1)} %bitcast.13), kind=kLoop, calls=%fused_computation.1 | loop fusion | flops 4653056 | bytes 9306112 | tf_op jit(solution)/shard_map/concatenate | solution.py:135
  124.7 22.9 %all-to-all-done = bf16[64,64,128]{2,0,1:T(8,128)(2,1)S(1)} async-done(((bf16[64,64,128]{2,0,1:T(8,128)(2,1)}), bf16[64,64,128]{2,0,1:T(8,128)(2,1)S(1)}, u32[]{:S(2)}, u32[]{:S(2)}) %all-to-all-start) | async-done | bytes 1048608 | tf_op jit(solution)/shard_map/all_to_all | solution.py:113
  147.6 1.0 copy-done.3
  148.6 24.7 %shard_map.55 = bf16[4096,128]{1,0:T(8,128)(2,1)} custom-call(s32[384]{0:T(512)} %min.32.index_ref, s32[384]{0:T(512)} %reshape.134.bound_ref, bf16[4096,128]{1,0:T(8,128)(2,1)} %bitcast.59, bf16[71,128,256]{2,1,0:T(8,128)(2,1)} %pad_maximum_fusion.pool_ref), custom_call_target="tpu_custom_call" | custom-call | flops 3221225472 | bytes 6750208 | tf_op jit(solution)/shard_map/pallas_call | solution.py:82
  173.8 2.7 %reduce.2 = bf16[4096,128]{1,0:T(8,128)(2,1)S(1)} reduce(bf16[4096,1,128]{2,0,1:T(8,128)(2,1)} %bitcast.56, bf16[]{:T(256)} %broadcast.189), dimensions={1}, to_apply=%copy.46.reduce_sub_computation | reduce | bytes 2097154 | tf_op jit(solution)/shard_map/reshape | solution.py:158
  176.7 60.0 %all_to_all.51 = bf16[64,2,4096]{2,1,0:T(2,128)(2,1)S(1)} all-to-all(bf16[64,2,4096]{2,1,0:T(2,128)(2,1)S(1)} %reshape.156), channel_id=1, replica_groups=mesh['grp'=8,'mem'=8,'ctx'=16] {'grp','mem'}, dimensions={0} | all-to-all | bytes 2097152 | tf_op jit(solution)/shard_map/all_to_all | solution.py:159
  236.7 1.0 reshape.157
  238.6 1.3 reshape.143
  (39 shorter events, 3.9 us)
Async XLA Ops:
  6.5 47.4 %copy-start = (s32[64,8]{0,1:T(8,128)S(1)}, s32[64,8]{0,1:T(8,128)}, u32[]{:S(2)}) copy-start(s32[64,8]{0,1:T(8,128)} %param.8) | copy-start | bytes 6148
  48.0 29.8 %all-to-all-start.2 = ((bf16[8,512,1,256]{3,1,2,0:T(8,128)(2,1)}), bf16[8,512,1,256]{3,1,2,0:T(8,128)(2,1)S(1)}, u32[]{:S(2)}, u32[]{:S(2)}) async-start(bf16[8,512,1,256]{3,1,2,0:T(8,128)(2,1)} %broadcast_in_dim.40), calls=%async_computation.2 | async-start | bytes 4194304 | tf_op jit(solution)/shard_map/all_to_all | solution.py:112
  53.9 67.2 %all-gather.3.cloned.1.call-start = ((), (), s32[]{:S(2)}) async-start(), calls=%async_computation.4 | async-start | bytes 2228224 | tf_op jit(solution)/shard_map/all_gather | solution.py:133
  77.8 1.3 copy-start.1
  79.1 3.2 %copy-start.2 = (bf16[1,64,8192]{2,1,0:T(8,128)(2,1)S(1)}, bf16[1,64,8192]{2,1,0:T(8,128)(2,1)}, u32[]{:S(2)}) copy-start(bf16[1,64,8192]{2,1,0:T(8,128)(2,1)} %param.5) | copy-start | bytes 3145732
  82.6 10.0 %copy-start.4 = (s32[64,4]{0,1:T(4,128)S(1)}, s32[64,4]{0,1:T(4,128)}, u32[]{:S(2)}) copy-start(s32[64,4]{0,1:T(4,128)} %param.9) | copy-start | bytes 3076
  84.2 63.4 %all-to-all-start = ((bf16[64,64,128]{2,0,1:T(8,128)(2,1)}), bf16[64,64,128]{2,0,1:T(8,128)(2,1)S(1)}, u32[]{:S(2)}, u32[]{:S(2)}) async-start(bf16[64,64,128]{2,0,1:T(8,128)(2,1)} %copy.42), calls=%async_computation | async-start | bytes 2097152 | tf_op jit(solution)/shard_map/all_to_all | solution.py:113
  93.6 13.8 %collective-permute-start = (bf16[896,256]{1,0:T(8,128)(2,1)}, bf16[896,256]{1,0:T(8,128)(2,1)}, u32[]{:S(2)}, u32[]{:S(2)}) collective-permute-start(bf16[896,256]{1,0:T(8,128)(2,1)} %slice.6), channel_id=1, source_target_pairs={{0,1},{1,2},{2,3},{3,4},{4,5},{5,6},{6,7},{7,8},{8,9},{9,10},{10,1... | collective-permute-start | bytes 1376264 | tf_op jit(solution)/shard_map/ppermute | solution.py:21
  147.6 1.0 copy-start.3
Sparse Core Ops, SparseCore 0:
  82.4 38.6 all-gather.2

commit v6 on v5

--- a/solution.py
+++ b/solution.py
@@ -56,7 +56,7 @@
         o_ref[part * BLK : (part + 1) * BLK, :] = (weighted / denominator).astype(o_ref.dtype)
 
 
-def attend(head_queries, key_pool, pool_index, bounds, per_step=2):
+def attend(head_queries, key_pool, pool_index, bounds, per_step=4):
     range_len, head_dim = head_queries.shape
     blocks = range_len // BLK
     candidates = pool_index.shape[1]
@@ -155,8 +155,10 @@
     )
     pool_index = jnp.concatenate([vertical_slots, slash_blocks - pool_base], axis=1)
     pool_index = jnp.clip(pool_index, 0, pool_size - 1).astype(jnp.int32)
-    head_output = attend(head_queries, key_pool, pool_index, bounds).reshape(range_len, 1, head_dim)
-    returned = lax.all_to_all(head_output, SEQ, split_axis=0, concat_axis=1, tiled=True)
+    head_output = attend(head_queries, key_pool, pool_index, bounds)
+    head_output = head_output.reshape(seq_count, tokens_dev, head_dim)
+    returned = lax.all_to_all(head_output, SEQ, split_axis=0, concat_axis=0, tiled=True)
+    returned = jnp.transpose(returned, (1, 0, 2))
     return returned.reshape(1, tokens_dev, seq_count * head_dim)
 
 

time: 247 us -> 241 us (0.976)
  the two profiles are of different devices: /device:TPU:48 before, /device:TPU:8 now
where the time goes in v6:
time: 241 us; the launch traced here: 240 us
  blocking collectives  98.2 us (41%)
  waiting for transfers between devices  70 us (29%)
  Pallas kernels  22.8 us (9%)
  starting transfers between devices  16.1 us (7%)
  local copies, waits for them, and re-layouts  15.3 us (6%)
  between operations  13.5 us (6%)
  other arithmetic  4.35 us (2%)
    all_to_all x1, blocking collectives, shards(): lax.all_to_all(head_output, SEQ, split_axis=0, concat_axis=0, tiled=True)  60.2 us
    all_to_all x1, blocking collectives, shards(): lax.all_to_all(local_pairs, 'grp', split_axis=1, concat_axis=0, tiled=True)  38 us
    all_to_all x1, waiting for transfers between devices, shards(): lax.all_to_all(group_pairs, 'mem', split_axis=0, concat_axis=0, tiled=True)  23.3 us
    pallas_call x1, Pallas kernels, attend(): pl.pallas_call(kernel, grid_spec=grid_spec, out_shape=jax.ShapeDtypeStruc...  22.8 us
    all_to_all x1, waiting for transfers between devices, shards(): lax.all_to_all(local_queries, SEQ, split_axis=1, concat_axis=0, tiled=True)  20.7 us
    all_gather x1, waiting for transfers between devices, shards(): vertical_pairs = lax.all_gather(taken_blocks, 'ctx', tiled=True)  16.4 us
    ppermute x1, waiting for transfers between devices, from_behind(): return lax.ppermute(block, axis, route)  9.54 us
    all_to_all x1, starting transfers between devices, shards(): lax.all_to_all(local_queries, SEQ, split_axis=1, concat_axis=0, tiled=True)  8.29 us
  transfers between devices with their start and end apart: 4, of which 4 were waited for; matrix products, arithmetic and copies ran while one was open for 4% of the time, Pallas kernels for 0%

profile of v6, /device:TPU:8, one launch (start us, length us, event | category | flops | bytes accessed | tf_op | source)
XLA Modules:
  0.0 240.3 jit_solution(3455062298601494021)
XLA Ops:
  6.5 0.9 copy.35
  7.5 0.9 copy.36
  8.5 38.0 %all_to_all.40 = bf16[64,8,256]{2,0,1:T(8,128)(2,1)S(1)} all-to-all(bf16[64,8,256]{2,0,1:T(8,128)(2,1)S(1)} %copy.29), channel_id=1, replica_groups=mesh['grp'=8,'mem'=8,'ctx'=16] {'grp'}, dimensions={1} | all-to-all | bytes 524288 | tf_op jit(solution)/shard_map/all_to_all | solution.py:109
  46.5 1.5 broadcast_in_dim.40
  48.0 5.9 %all-to-all-start.2 = ((bf16[8,512,1,256]{3,1,2,0:T(8,128)(2,1)}), bf16[8,512,1,256]{3,1,2,0:T(8,128)(2,1)S(1)}, u32[]{:S(2)}, u32[]{:S(2)}) async-start(bf16[8,512,1,256]{3,1,2,0:T(8,128)(2,1)} %broadcast_in_dim.40), calls=%async_computation.2 | async-start | bytes 4194304 | tf_op jit(solution)/shard_map/all_to_all | solution.py:112
  54.4 23.3 %all-to-all-done.2 = bf16[8,512,1,256]{3,1,2,0:T(8,128)(2,1)S(1)} async-done(((bf16[8,512,1,256]{3,1,2,0:T(8,128)(2,1)}), bf16[8,512,1,256]{3,1,2,0:T(8,128)(2,1)S(1)}, u32[]{:S(2)}, u32[]{:S(2)}) %all-to-all-start.2) | async-done | bytes 2097184 | tf_op jit(solution)/shard_map/all_to_all | solution.py:112
  77.8 1.3 copy-done.1
  79.1 1.8 copy.30
  80.9 1.2 gather_fusion
  82.5 1.6 copy.28
  84.1 8.3 %all-to-all-start = ((bf16[64,64,128]{2,0,1:T(8,128)(2,1)}), bf16[64,64,128]{2,0,1:T(8,128)(2,1)S(1)}, u32[]{:S(2)}, u32[]{:S(2)}) async-start(bf16[64,64,128]{2,0,1:T(8,128)(2,1)} %copy.28), calls=%async_computation | async-start | bytes 2097152 | tf_op jit(solution)/shard_map/all_to_all | solution.py:113
  92.6 0.8 slice.6
  93.4 1.9 collective-permute-start
  95.7 0.7 min.32.index_ref
  96.5 0.7 reshape.133.bound_ref
  97.2 9.5 %collective-permute-done = bf16[896,256]{1,0:T(8,128)(2,1)} collective-permute-done((bf16[896,256]{1,0:T(8,128)(2,1)}, bf16[896,256]{1,0:T(8,128)(2,1)}, u32[]{:S(2)}, u32[]{:S(2)}) %collective-permute-start) | collective-permute-done | bytes 458784 | tf_op jit(solution)/shard_map/ppermute | solution.py:21
  106.7 16.4 %all-gather.3.cloned.1.call-done = bf16[32,128,256]{2,1,0:T(8,128)(2,1)} async-done(((bf16[2,128,256]{2,1,0:T(8,128)(2,1)}), bf16[32,128,256]{2,1,0:T(8,128)(2,1)}) %all-gather.3.cloned.1.call-update) | async-done | bytes 2097168 | tf_op jit(solution)/shard_map/all_gather | solution.py:133
  123.1 3.7 %pad_maximum_fusion.pool_ref = bf16[71,128,256]{2,1,0:T(8,128)(2,1)} fusion(bf16[32,128,256]{2,1,0:T(8,128)(2,1)} %all-gather.3.cloned.1.call-done, bf16[32,128,256]{2,1,0:T(8,128)(2,1)S(1)} %bitcast.46, bf16[7,128,256]{2,1,0:T(8,128)(2,1)} %bitcast.13), kind=kLoop, calls=%fused_computation.1 | loop fusion | flops 4653056 | bytes 9306112 | tf_op jit(solution)/shard_map/concatenate | solution.py:135
  126.8 20.7 %all-to-all-done = bf16[64,64,128]{2,0,1:T(8,128)(2,1)S(1)} async-done(((bf16[64,64,128]{2,0,1:T(8,128)(2,1)}), bf16[64,64,128]{2,0,1:T(8,128)(2,1)S(1)}, u32[]{:S(2)}, u32[]{:S(2)}) %all-to-all-start) | async-done | bytes 1048608 | tf_op jit(solution)/shard_map/all_to_all | solution.py:113
  147.5 1.0 copy-done.3
  148.5 22.8 %shard_map.55 = bf16[4096,128]{1,0:T(8,128)(2,1)} custom-call(s32[384]{0:T(512)} %min.32.index_ref, s32[384]{0:T(512)} %reshape.133.bound_ref, bf16[4096,128]{1,0:T(8,128)(2,1)} %bitcast.52, bf16[71,128,256]{2,1,0:T(8,128)(2,1)} %pad_maximum_fusion.pool_ref), custom_call_target="tpu_custom_call" | custom-call | flops 3221225472 | bytes 6750208 | tf_op jit(solution)/shard_map/pallas_call | solution.py:82
  171.3 60.2 %all_to_all.41 = bf16[64,64,128]{2,1,0:T(8,128)(2,1)S(1)} all-to-all(bf16[64,64,128]{2,1,0:T(8,128)(2,1)} %bitcast.53), channel_id=1, replica_groups=mesh['grp'=8,'mem'=8,'ctx'=16] {'grp','mem'}, dimensions={0} | all-to-all | bytes 2097152 | tf_op jit(solution)/shard_map/all_to_all | solution.py:160
  231.5 0.7 copy.32
  232.2 1.3 reshape.142
  (34 shorter events, 1.6 us)
Async XLA Ops:
  6.5 47.4 %copy-start = (s32[64,8]{0,1:T(8,128)S(1)}, s32[64,8]{0,1:T(8,128)}, u32[]{:S(2)}) copy-start(s32[64,8]{0,1:T(8,128)} %param.8) | copy-start | bytes 6148
  48.0 29.8 %all-to-all-start.2 = ((bf16[8,512,1,256]{3,1,2,0:T(8,128)(2,1)}), bf16[8,512,1,256]{3,1,2,0:T(8,128)(2,1)S(1)}, u32[]{:S(2)}, u32[]{:S(2)}) async-start(bf16[8,512,1,256]{3,1,2,0:T(8,128)(2,1)} %broadcast_in_dim.40), calls=%async_computation.2 | async-start | bytes 4194304 | tf_op jit(solution)/shard_map/all_to_all | solution.py:112
  53.9 69.3 %all-gather.3.cloned.1.call-start = ((), (), s32[]{:S(2)}) async-start(), calls=%async_computation.4 | async-start | bytes 2228224 | tf_op jit(solution)/shard_map/all_gather | solution.py:133
  77.8 1.3 copy-start.1
  79.1 3.1 %copy-start.2 = (bf16[1,64,8192]{2,1,0:T(8,128)(2,1)S(1)}, bf16[1,64,8192]{2,1,0:T(8,128)(2,1)}, u32[]{:S(2)}) copy-start(bf16[1,64,8192]{2,1,0:T(8,128)(2,1)} %param.5) | copy-start | bytes 3145732
  82.4 10.0 %copy-start.4 = (s32[64,4]{0,1:T(4,128)S(1)}, s32[64,4]{0,1:T(4,128)}, u32[]{:S(2)}) copy-start(s32[64,4]{0,1:T(4,128)} %param.9) | copy-start | bytes 3076
  84.1 63.4 %all-to-all-start = ((bf16[64,64,128]{2,0,1:T(8,128)(2,1)}), bf16[64,64,128]{2,0,1:T(8,128)(2,1)S(1)}, u32[]{:S(2)}, u32[]{:S(2)}) async-start(bf16[64,64,128]{2,0,1:T(8,128)(2,1)} %copy.28), calls=%async_computation | async-start | bytes 2097152 | tf_op jit(solution)/shard_map/all_to_all | solution.py:113
  93.4 13.3 %collective-permute-start = (bf16[896,256]{1,0:T(8,128)(2,1)}, bf16[896,256]{1,0:T(8,128)(2,1)}, u32[]{:S(2)}, u32[]{:S(2)}) collective-permute-start(bf16[896,256]{1,0:T(8,128)(2,1)} %slice.6), channel_id=1, source_target_pairs={{0,1},{1,2},{2,3},{3,4},{4,5},{5,6},{6,7},{7,8},{8,9},{9,10},{10,1... | collective-permute-start | bytes 1376264 | tf_op jit(solution)/shard_map/ppermute | solution.py:21
  147.5 1.0 copy-start.3
Sparse Core Ops, SparseCore 0:
  82.3 40.7 all-gather.2

commit v7 on v6

--- a/solution.py
+++ b/solution.py
@@ -38,22 +38,26 @@
         queries = q_ref[part * BLK : (part + 1) * BLK, :]
         scores = (
             lax.dot_general(
-                queries, key_ref[...], (((1,), (1,)), ((), ())), preferred_element_type=jnp.float32
+                key_ref[...], queries, (((1,), (1,)), ((), ())), preferred_element_type=jnp.float32
             )
             * scale
         )
         masked = []
         for k in range(candidates):
             bound = bound_ref[block * candidates + k]
-            masked.append(jnp.where(offset <= bound, scores[:, k * BLK : (k + 1) * BLK], -1e30))
-        scores = jnp.concatenate(masked, axis=1)
-        row_max = jnp.max(scores, axis=1, keepdims=True)
-        weights = jnp.exp(scores - row_max)
-        denominator = jnp.sum(weights, axis=1, keepdims=True)
-        weighted = jnp.dot(
-            weights.astype(jnp.bfloat16), value_ref[...], preferred_element_type=jnp.float32
+            masked.append(jnp.where(-offset <= bound, scores[k * BLK : (k + 1) * BLK, :], -1e30))
+        scores = jnp.concatenate(masked, axis=0)
+        col_max = jnp.max(scores, axis=0, keepdims=True)
+        weights = jnp.exp(scores - col_max)
+        denominator = jnp.sum(weights, axis=0, keepdims=True)
+        weighted = lax.dot_general(
+            weights.astype(jnp.bfloat16),
+            value_ref[...],
+            (((0,), (0,)), ((), ())),
+            preferred_element_type=jnp.float32,
         )
-        o_ref[part * BLK : (part + 1) * BLK, :] = (weighted / denominator).astype(o_ref.dtype)
+        result = (weighted.T / denominator).astype(o_ref.dtype)
+        o_ref[part * BLK : (part + 1) * BLK, :] = result.T
 
 
 def attend(head_queries, key_pool, pool_index, bounds, per_step=4):

time: 241 us -> 242 us (level)
  the two profiles are of different devices: /device:TPU:8 before, /device:TPU:40 now
where the time goes in v7:
time: 242 us; the launch traced here: 241 us
  blocking collectives  98.2 us (41%)
  waiting for transfers between devices  70 us (29%)
  Pallas kernels  24 us (10%)
  starting transfers between devices  16.1 us (7%)
  local copies, waits for them, and re-layouts  15.3 us (6%)
  between operations  13.5 us (6%)
  other arithmetic  4.35 us (2%)
    all_to_all x1, blocking collectives, shards(): lax.all_to_all(head_output, SEQ, split_axis=0, concat_axis=0, tiled=True)  60.2 us
    all_to_all x1, blocking collectives, shards(): lax.all_to_all(local_pairs, 'grp', split_axis=1, concat_axis=0, tiled=True)  38 us
    pallas_call x1, Pallas kernels, attend(): pl.pallas_call(kernel, grid_spec=grid_spec, out_shape=jax.ShapeDtypeStruc...  24 us
    all_to_all x1, waiting for transfers between devices, shards(): lax.all_to_all(group_pairs, 'mem', split_axis=0, concat_axis=0, tiled=True)  23.3 us
    all_to_all x1, waiting for transfers between devices, shards(): lax.all_to_all(local_queries, SEQ, split_axis=1, concat_axis=0, tiled=True)  22.4 us
    all_gather x1, waiting for transfers between devices, shards(): vertical_pairs = lax.all_gather(taken_blocks, 'ctx', tiled=True)  14.1 us
    ppermute x1, waiting for transfers between devices, from_behind(): return lax.ppermute(block, axis, route)  10.2 us
    all_to_all x1, starting transfers between devices, shards(): lax.all_to_all(local_queries, SEQ, split_axis=1, concat_axis=0, tiled=True)  8.29 us
  transfers between devices with their start and end apart: 4, of which 4 were waited for; matrix products, arithmetic and copies ran while one was open for 4% of the time, Pallas kernels for 0%

profile of v7, /device:TPU:40, one launch (start us, length us, event | category | flops | bytes accessed | tf_op | source)
XLA Modules:
  0.0 241.5 jit_solution(9903852889452264610)
XLA Ops:
  6.5 0.9 copy.35
  7.5 0.9 copy.36
  8.5 38.0 %all_to_all.40 = bf16[64,8,256]{2,0,1:T(8,128)(2,1)S(1)} all-to-all(bf16[64,8,256]{2,0,1:T(8,128)(2,1)S(1)} %copy.29), channel_id=1, replica_groups=mesh['grp'=8,'mem'=8,'ctx'=16] {'grp'}, dimensions={1} | all-to-all | bytes 524288 | tf_op jit(solution)/shard_map/all_to_all | solution.py:113
  46.5 1.5 broadcast_in_dim.40
  48.0 5.9 %all-to-all-start.2 = ((bf16[8,512,1,256]{3,1,2,0:T(8,128)(2,1)}), bf16[8,512,1,256]{3,1,2,0:T(8,128)(2,1)S(1)}, u32[]{:S(2)}, u32[]{:S(2)}) async-start(bf16[8,512,1,256]{3,1,2,0:T(8,128)(2,1)} %broadcast_in_dim.40), calls=%async_computation.2 | async-start | bytes 4194304 | tf_op jit(solution)/shard_map/all_to_all | solution.py:116
  54.4 23.3 %all-to-all-done.2 = bf16[8,512,1,256]{3,1,2,0:T(8,128)(2,1)S(1)} async-done(((bf16[8,512,1,256]{3,1,2,0:T(8,128)(2,1)}), bf16[8,512,1,256]{3,1,2,0:T(8,128)(2,1)S(1)}, u32[]{:S(2)}, u32[]{:S(2)}) %all-to-all-start.2) | async-done | bytes 2097184 | tf_op jit(solution)/shard_map/all_to_all | solution.py:116
  77.8 1.3 copy-done.1
  79.1 1.8 copy.30
  80.9 1.2 gather_fusion
  82.5 1.6 copy.28
  84.1 8.3 %all-to-all-start = ((bf16[64,64,128]{2,0,1:T(8,128)(2,1)}), bf16[64,64,128]{2,0,1:T(8,128)(2,1)S(1)}, u32[]{:S(2)}, u32[]{:S(2)}) async-start(bf16[64,64,128]{2,0,1:T(8,128)(2,1)} %copy.28), calls=%async_computation | async-start | bytes 2097152 | tf_op jit(solution)/shard_map/all_to_all | solution.py:117
  92.6 0.8 slice.6
  93.4 1.9 collective-permute-start
  95.7 0.7 min.32.index_ref
  96.5 0.7 reshape.133.bound_ref
  97.2 10.2 %collective-permute-done = bf16[896,256]{1,0:T(8,128)(2,1)} collective-permute-done((bf16[896,256]{1,0:T(8,128)(2,1)}, bf16[896,256]{1,0:T(8,128)(2,1)}, u32[]{:S(2)}, u32[]{:S(2)}) %collective-permute-start) | collective-permute-done | bytes 458784 | tf_op jit(solution)/shard_map/ppermute | solution.py:21
  107.4 14.1 %all-gather.3.cloned.1.call-done = bf16[32,128,256]{2,1,0:T(8,128)(2,1)} async-done(((bf16[2,128,256]{2,1,0:T(8,128)(2,1)}), bf16[32,128,256]{2,1,0:T(8,128)(2,1)}) %all-gather.3.cloned.1.call-update) | async-done | bytes 2097168 | tf_op jit(solution)/shard_map/all_gather | solution.py:137
  121.4 3.7 %pad_maximum_fusion.pool_ref = bf16[71,128,256]{2,1,0:T(8,128)(2,1)} fusion(bf16[32,128,256]{2,1,0:T(8,128)(2,1)} %all-gather.3.cloned.1.call-done, bf16[32,128,256]{2,1,0:T(8,128)(2,1)S(1)} %bitcast.46, bf16[7,128,256]{2,1,0:T(8,128)(2,1)} %bitcast.13), kind=kLoop, calls=%fused_computation.1 | loop fusion | flops 4653056 | bytes 9306112 | tf_op jit(solution)/shard_map/concatenate | solution.py:139
  125.1 22.4 %all-to-all-done = bf16[64,64,128]{2,0,1:T(8,128)(2,1)S(1)} async-done(((bf16[64,64,128]{2,0,1:T(8,128)(2,1)}), bf16[64,64,128]{2,0,1:T(8,128)(2,1)S(1)}, u32[]{:S(2)}, u32[]{:S(2)}) %all-to-all-start) | async-done | bytes 1048608 | tf_op jit(solution)/shard_map/all_to_all | solution.py:117
  147.5 1.0 copy-done.3
  148.5 24.0 %shard_map.55 = bf16[4096,128]{1,0:T(8,128)(2,1)} custom-call(s32[384]{0:T(512)} %min.32.index_ref, s32[384]{0:T(512)} %reshape.133.bound_ref, bf16[4096,128]{1,0:T(8,128)(2,1)} %bitcast.52, bf16[71,128,256]{2,1,0:T(8,128)(2,1)} %pad_maximum_fusion.pool_ref), custom_call_target="tpu_custom_call" | custom-call | flops 3221225472 | bytes 6750208 | tf_op jit(solution)/shard_map/pallas_call | solution.py:86
  172.5 60.2 %all_to_all.41 = bf16[64,64,128]{2,1,0:T(8,128)(2,1)S(1)} all-to-all(bf16[64,64,128]{2,1,0:T(8,128)(2,1)} %bitcast.53), channel_id=1, replica_groups=mesh['grp'=8,'mem'=8,'ctx'=16] {'grp','mem'}, dimensions={0} | all-to-all | bytes 2097152 | tf_op jit(solution)/shard_map/all_to_all | solution.py:164
  232.7 0.7 copy.32
  233.3 1.3 reshape.142
  (34 shorter events, 1.6 us)
Async XLA Ops:
  6.5 47.4 %copy-start = (s32[64,8]{0,1:T(8,128)S(1)}, s32[64,8]{0,1:T(8,128)}, u32[]{:S(2)}) copy-start(s32[64,8]{0,1:T(8,128)} %param.8) | copy-start | bytes 6148
  48.0 29.8 %all-to-all-start.2 = ((bf16[8,512,1,256]{3,1,2,0:T(8,128)(2,1)}), bf16[8,512,1,256]{3,1,2,0:T(8,128)(2,1)S(1)}, u32[]{:S(2)}, u32[]{:S(2)}) async-start(bf16[8,512,1,256]{3,1,2,0:T(8,128)(2,1)} %broadcast_in_dim.40), calls=%async_computation.2 | async-start | bytes 4194304 | tf_op jit(solution)/shard_map/all_to_all | solution.py:116
  53.9 67.6 %all-gather.3.cloned.1.call-start = ((), (), s32[]{:S(2)}) async-start(), calls=%async_computation.4 | async-start | bytes 2228224 | tf_op jit(solution)/shard_map/all_gather | solution.py:137
  77.8 1.3 copy-start.1
  79.1 3.1 %copy-start.2 = (bf16[1,64,8192]{2,1,0:T(8,128)(2,1)S(1)}, bf16[1,64,8192]{2,1,0:T(8,128)(2,1)}, u32[]{:S(2)}) copy-start(bf16[1,64,8192]{2,1,0:T(8,128)(2,1)} %param.5) | copy-start | bytes 3145732
  82.4 10.0 %copy-start.4 = (s32[64,4]{0,1:T(4,128)S(1)}, s32[64,4]{0,1:T(4,128)}, u32[]{:S(2)}) copy-start(s32[64,4]{0,1:T(4,128)} %param.9) | copy-start | bytes 3076
  84.1 63.4 %all-to-all-start = ((bf16[64,64,128]{2,0,1:T(8,128)(2,1)}), bf16[64,64,128]{2,0,1:T(8,128)(2,1)S(1)}, u32[]{:S(2)}, u32[]{:S(2)}) async-start(bf16[64,64,128]{2,0,1:T(8,128)(2,1)} %copy.28), calls=%async_computation | async-start | bytes 2097152 | tf_op jit(solution)/shard_map/all_to_all | solution.py:117
  93.4 13.9 %collective-permute-start = (bf16[896,256]{1,0:T(8,128)(2,1)}, bf16[896,256]{1,0:T(8,128)(2,1)}, u32[]{:S(2)}, u32[]{:S(2)}) collective-permute-start(bf16[896,256]{1,0:T(8,128)(2,1)} %slice.6), channel_id=1, source_target_pairs={{0,1},{1,2},{2,3},{3,4},{4,5},{5,6},{6,7},{7,8},{8,9},{9,10},{10,1... | collective-permute-start | bytes 1376264 | tf_op jit(solution)/shard_map/ppermute | solution.py:21
  147.5 1.0 copy-start.3
Sparse Core Ops, SparseCore 0:
  82.3 39.1 all-gather.2

commit v8 on v6

--- a/solution.py
+++ b/solution.py
@@ -56,7 +56,7 @@
         o_ref[part * BLK : (part + 1) * BLK, :] = (weighted / denominator).astype(o_ref.dtype)
 
 
-def attend(head_queries, key_pool, pool_index, bounds, per_step=4):
+def attend(head_queries, key_pool, pool_index, bounds, per_step=8):
     range_len, head_dim = head_queries.shape
     blocks = range_len // BLK
     candidates = pool_index.shape[1]
@@ -108,11 +108,11 @@
     )
     group_pairs = lax.all_to_all(local_pairs, "grp", split_axis=1, concat_axis=0, tiled=True)
     members = lax.axis_size("mem")
-    group_pairs = jnp.broadcast_to(group_pairs[None], (members,) + group_pairs.shape)
-    group_pairs = lax.all_to_all(group_pairs, "mem", split_axis=0, concat_axis=0, tiled=True)
+    groups = group_pairs.shape[0] // tokens_dev
+    group_pairs = group_pairs.reshape(1, groups, 1, tokens_dev, 2 * head_dim)
+    group_pairs = jnp.broadcast_to(group_pairs, (members,) + group_pairs.shape[1:])
+    head_pairs = lax.all_to_all(group_pairs, "mem", split_axis=0, concat_axis=2, tiled=True)
     head_queries = lax.all_to_all(local_queries, SEQ, split_axis=1, concat_axis=0, tiled=True)
-    group_pairs = group_pairs.reshape(members, kv_heads, tokens_dev, 2 * head_dim)
-    head_pairs = jnp.transpose(group_pairs, (1, 0, 2, 3))
     range_len = tokens_dev * seq_count
     blocks_slab = range_len // BLK
     head_queries = head_queries.reshape(range_len, head_dim)

time: 241 us -> 239 us (level)
  no operation moved by 1% of the time
where the time goes in v8:
time: 239 us; the launch traced here: 238 us
  blocking collectives  98.2 us (41%)
  waiting for transfers between devices  70.1 us (29%)
  Pallas kernels  21.9 us (9%)
  starting transfers between devices  16.1 us (7%)
  local copies, waits for them, and re-layouts  14 us (6%)
  between operations  13.5 us (6%)
  other arithmetic  4.27 us (2%)
    all_to_all x1, blocking collectives, shards(): lax.all_to_all(head_output, SEQ, split_axis=0, concat_axis=0, tiled=True)  60.2 us
    all_to_all x1, blocking collectives, shards(): lax.all_to_all(local_pairs, 'grp', split_axis=1, concat_axis=0, tiled=True)  38 us
    all_to_all x1, waiting for transfers between devices, shards(): lax.all_to_all(group_pairs, 'mem', split_axis=0, concat_axis=2, tiled=True)  23.4 us
    pallas_call x1, Pallas kernels, attend(): pl.pallas_call(kernel, grid_spec=grid_spec, out_shape=jax.ShapeDtypeStruc...  21.9 us
    all_to_all x1, waiting for transfers between devices, shards(): lax.all_to_all(local_queries, SEQ, split_axis=1, concat_axis=0, tiled=True)  20.7 us
    all_gather x1, waiting for transfers between devices, shards(): vertical_pairs = lax.all_gather(taken_blocks, 'ctx', tiled=True)  16.4 us
    ppermute x1, waiting for transfers between devices, from_behind(): return lax.ppermute(block, axis, route)  9.53 us
    all_to_all x1, starting transfers between devices, shards(): lax.all_to_all(local_queries, SEQ, split_axis=1, concat_axis=0, tiled=True)  8.29 us
  transfers between devices with their start and end apart: 4, of which 4 were waited for; matrix products, arithmetic and copies ran while one was open for 4% of the time, Pallas kernels for 0%

profile of v8, /device:TPU:8, one launch (start us, length us, event | category | flops | bytes accessed | tf_op | source)
XLA Modules:
  0.0 238.1 jit_solution(13122972295390680502)
XLA Ops:
  6.5 0.9 copy.32
  7.5 0.9 copy.33
  8.5 38.0 %all_to_all.50 = bf16[64,8,256]{2,0,1:T(8,128)(2,1)S(1)} all-to-all(bf16[64,8,256]{2,0,1:T(8,128)(2,1)S(1)} %copy.27), channel_id=1, replica_groups=mesh['grp'=8,'mem'=8,'ctx'=16] {'grp'}, dimensions={1} | all-to-all | bytes 524288 | tf_op jit(solution)/shard_map/all_to_all | solution.py:109
  46.5 1.6 broadcast_in_dim.40
  48.1 5.9 %all-to-all-start.2 = ((bf16[8,8,1,64,256]{4,3,1,2,0:T(8,128)(2,1)}), bf16[8,8,1,64,256]{4,3,1,2,0:T(8,128)(2,1)}, u32[]{:S(2)}, u32[]{:S(2)}) async-start(bf16[8,8,1,64,256]{4,3,1,2,0:T(8,128)(2,1)} %broadcast_in_dim.40), calls=%async_computation.2 | async-start | bytes 4194304 | tf_op jit(solution)/shard_map/all_to_all | solution.py:114
  54.6 23.4 %all-to-all-done.2 = bf16[8,8,1,64,256]{4,3,1,2,0:T(8,128)(2,1)} async-done(((bf16[8,8,1,64,256]{4,3,1,2,0:T(8,128)(2,1)}), bf16[8,8,1,64,256]{4,3,1,2,0:T(8,128)(2,1)}, u32[]{:S(2)}, u32[]{:S(2)}) %all-to-all-start.2) | async-done | bytes 2097184 | tf_op jit(solution)/shard_map/all_to_all | solution.py:114
  78.0 1.7 copy.28
  79.7 1.2 gather_fusion
  81.0 0.3 copy.31
  81.2 1.6 copy.26
  82.9 8.3 %all-to-all-start = ((bf16[64,64,128]{2,0,1:T(8,128)(2,1)}), bf16[64,64,128]{2,0,1:T(8,128)(2,1)S(1)}, u32[]{:S(2)}, u32[]{:S(2)}) async-start(bf16[64,64,128]{2,0,1:T(8,128)(2,1)} %copy.26), calls=%async_computation | async-start | bytes 2097152 | tf_op jit(solution)/shard_map/all_to_all | solution.py:115
  91.4 0.8 slice.6
  92.2 1.9 collective-permute-start
  94.5 0.7 min.32.index_ref
  95.3 0.7 reshape.133.bound_ref
  96.0 9.5 %collective-permute-done = bf16[896,256]{1,0:T(8,128)(2,1)} collective-permute-done((bf16[896,256]{1,0:T(8,128)(2,1)}, bf16[896,256]{1,0:T(8,128)(2,1)}, u32[]{:S(2)}, u32[]{:S(2)}) %collective-permute-start) | collective-permute-done | bytes 458784 | tf_op jit(solution)/shard_map/ppermute | solution.py:21
  105.5 16.4 %all-gather.3.cloned.1.call-done = bf16[32,128,256]{2,1,0:T(8,128)(2,1)} async-done(((bf16[2,128,256]{2,1,0:T(8,128)(2,1)}), bf16[32,128,256]{2,1,0:T(8,128)(2,1)}) %all-gather.3.cloned.1.call-update) | async-done | bytes 2097168 | tf_op jit(solution)/shard_map/all_gather | solution.py:133
  121.9 3.6 %pad_maximum_fusion.pool_ref = bf16[71,128,256]{2,1,0:T(8,128)(2,1)} fusion(bf16[32,128,256]{2,1,0:T(8,128)(2,1)} %all-gather.3.cloned.1.call-done, bf16[32,128,256]{2,1,0:T(8,128)(2,1)S(1)} %bitcast.48, bf16[7,128,256]{2,1,0:T(8,128)(2,1)} %bitcast.13), kind=kLoop, calls=%fused_computation.1 | loop fusion | flops 4653056 | bytes 9306112 | tf_op jit(solution)/shard_map/concatenate | solution.py:135
  125.5 20.7 %all-to-all-done = bf16[64,64,128]{2,0,1:T(8,128)(2,1)S(1)} async-done(((bf16[64,64,128]{2,0,1:T(8,128)(2,1)}), bf16[64,64,128]{2,0,1:T(8,128)(2,1)S(1)}, u32[]{:S(2)}, u32[]{:S(2)}) %all-to-all-start) | async-done | bytes 1048608 | tf_op jit(solution)/shard_map/all_to_all | solution.py:115
  146.3 1.0 copy-done.2
  147.2 21.9 %shard_map.55 = bf16[4096,128]{1,0:T(8,128)(2,1)} custom-call(s32[384]{0:T(512)} %min.32.index_ref, s32[384]{0:T(512)} %reshape.133.bound_ref, bf16[4096,128]{1,0:T(8,128)(2,1)} %bitcast.53, bf16[71,128,256]{2,1,0:T(8,128)(2,1)} %pad_maximum_fusion.pool_ref), custom_call_target="tpu_custom_call" | custom-call | flops 3221225472 | bytes 6750208 | tf_op jit(solution)/shard_map/pallas_call | solution.py:82
  169.1 60.2 %all_to_all.51 = bf16[64,64,128]{2,1,0:T(8,128)(2,1)S(1)} all-to-all(bf16[64,64,128]{2,1,0:T(8,128)(2,1)} %bitcast.54), channel_id=1, replica_groups=mesh['grp'=8,'mem'=8,'ctx'=16] {'grp','mem'}, dimensions={0} | all-to-all | bytes 2097152 | tf_op jit(solution)/shard_map/all_to_all | solution.py:160
  229.3 0.7 copy.29
  230.0 1.3 reshape.141
  (32 shorter events, 1.3 us)
Async XLA Ops:
  6.5 47.5 %copy-start = (s32[64,8]{0,1:T(8,128)S(1)}, s32[64,8]{0,1:T(8,128)}, u32[]{:S(2)}) copy-start(s32[64,8]{0,1:T(8,128)} %param.8) | copy-start | bytes 6148
  48.1 29.9 %all-to-all-start.2 = ((bf16[8,8,1,64,256]{4,3,1,2,0:T(8,128)(2,1)}), bf16[8,8,1,64,256]{4,3,1,2,0:T(8,128)(2,1)}, u32[]{:S(2)}, u32[]{:S(2)}) async-start(bf16[8,8,1,64,256]{4,3,1,2,0:T(8,128)(2,1)} %broadcast_in_dim.40), calls=%async_computation.2 | async-start | bytes 4194304 | tf_op jit(solution)/shard_map/all_to_all | solution.py:114
  54.0 68.0 %all-gather.3.cloned.1.call-start = ((), (), s32[]{:S(2)}) async-start(), calls=%async_computation.4 | async-start | bytes 2228224 | tf_op jit(solution)/shard_map/all_gather | solution.py:133
  54.5 26.4 %copy-start.1 = (bf16[1,64,8192]{2,1,0:T(8,128)(2,1)S(1)}, bf16[1,64,8192]{2,1,0:T(8,128)(2,1)}, u32[]{:S(2)}) copy-start(bf16[1,64,8192]{2,1,0:T(8,128)(2,1)} %param.5) | copy-start | bytes 3145732
  81.2 10.0 %copy-start.3 = (s32[64,4]{0,1:T(4,128)S(1)}, s32[64,4]{0,1:T(4,128)}, u32[]{:S(2)}) copy-start(s32[64,4]{0,1:T(4,128)} %param.9) | copy-start | bytes 3076
  82.9 63.4 %all-to-all-start = ((bf16[64,64,128]{2,0,1:T(8,128)(2,1)}), bf16[64,64,128]{2,0,1:T(8,128)(2,1)S(1)}, u32[]{:S(2)}, u32[]{:S(2)}) async-start(bf16[64,64,128]{2,0,1:T(8,128)(2,1)} %copy.26), calls=%async_computation | async-start | bytes 2097152 | tf_op jit(solution)/shard_map/all_to_all | solution.py:115
  92.2 13.3 %collective-permute-start = (bf16[896,256]{1,0:T(8,128)(2,1)}, bf16[896,256]{1,0:T(8,128)(2,1)}, u32[]{:S(2)}, u32[]{:S(2)}) collective-permute-start(bf16[896,256]{1,0:T(8,128)(2,1)} %slice.6), channel_id=1, source_target_pairs={{0,1},{1,2},{2,3},{3,4},{4,5},{5,6},{6,7},{7,8},{8,9},{9,10},{10,1... | collective-permute-start | bytes 1376264 | tf_op jit(solution)/shard_map/ppermute | solution.py:21
  146.3 1.0 copy-start.2
Sparse Core Ops, SparseCore 0:
  81.1 40.7 all-gather.2
